TPU v7x, 256 devices: a whole 4x4x8 slice. The times are simulated.
256 devices in a mesh: term: 4 (over x), sec: 64 (over y, z, core).
Axes of the slice: x: 4, y: 4, z: 8, core: 2. Of those that a mesh axis runs over, the one named last changes fastest.
Arguments:
- vectors: bfloat16 [1, 4096, 256, 256], P(None, 'sec'), may hold values from -6 to 6
- left_env: bfloat16 [4, 128, 256, 256], P('term', 'sec'), may hold values from -0.375 to 0.375
- right_env: bfloat16 [4, 128, 256, 256], P('term', 'sec'), may hold values from -0.375 to 0.375
- left_sector: int32 [64, 64], P('sec'), may hold values from 0 to 1
- right_sector: int32 [64, 64], P('sec'), may hold values from 0 to 1
- tile_count: int32 [64], P('sec'), may hold values from 1 to 64, 3072 in all
- departure: int32 [64, 64], P('sec'), may hold values from 0 to 63, each once within a row
- arrival: int32 [64, 64], P('sec'), may hold values from 0 to 63, each once within a row
Outputs:
- sigma: bfloat16 [1, 4096, 256, 256], P(None, 'sec', 'term')
Inputs may be any that keep to these rules, and one draw needn't show every extreme that they name: `tile_count`: every sec index owns some tile slots that are live; the busiest left owner has all 64 slots live. `departure`: each row is a permutation of the slots. `arrival`: each row is a permutation of the slots.
All inputs are finite; a program needn't handle non-finite values. No bound on the sum of `tile_count` on one device may be relied on, other than what follows from the above.
Results may differ from a plain program's by a relative error of at most 0.015.
Values may be sent and summed in bfloat16 or wider, within the bound.
No kernel may reach another device: no remote copies, remote signals or barrier semaphores. Data moves between devices by JAX's collectives and lax.ppermute only.
A program may use at most 128 MiB of HBM per device.

v0:
```python
import jax
import jax.numpy as jnp
from jax import lax
from jax.sharding import PartitionSpec as P


def pick_blocks(table, index):
    picked = jnp.zeros((index.shape[0],) + table.shape[1:], table.dtype)
    for sector in range(table.shape[0]):
        picked = jnp.where((index == sector)[:, None, None], table[sector][None], picked)
    return picked


def on_device(
    vectors, left_env, right_env, left_sector, right_sector, tile_count, departure, arrival
):
    n_sec = lax.axis_size("sec")
    n_vecs = vectors.shape[0]
    tiles_dev = vectors.shape[1]
    width = vectors.shape[3]
    per_peer = tiles_dev // n_sec
    live = (jnp.arange(tiles_dev, dtype=jnp.int32) < tile_count[0]).astype(jnp.bfloat16)
    masked = vectors * live[None, :, None, None]
    left_blocks = pick_blocks(left_env[0], left_sector[0])
    applied = jnp.einsum(
        "kij,vkjl->vkil", left_blocks, masked, preferred_element_type=jnp.float32
    ).astype(jnp.bfloat16)
    outgoing = jnp.take(applied, departure[0], axis=1)
    outgoing = outgoing.reshape(n_vecs, n_sec, per_peer, width, width)
    incoming = lax.all_to_all(outgoing, "sec", split_axis=1, concat_axis=1, tiled=True)
    incoming = incoming.reshape(n_vecs, tiles_dev, width, width)
    placed = jnp.take(incoming, arrival[0], axis=1)
    right_blocks = pick_blocks(right_env[0], right_sector[0])
    contrib = jnp.einsum(
        "vkil,kml->vkim", placed, right_blocks, preferred_element_type=jnp.float32
    ).astype(jnp.bfloat16)
    summed = lax.psum_scatter(
        contrib.astype(jnp.float32).astype(jnp.bfloat16), "term", scatter_dimension=2, tiled=True
    )
    return summed


def solution(mesh):
    in_specs = (
        P(None, "sec", None, None),
        P("term", "sec", None, None),
        P("term", "sec", None, None),
        P("sec", None),
        P("sec", None),
        P("sec"),
        P("sec", None),
        P("sec", None),
    )
    out_specs = P(None, "sec", "term", None)
    return jax.shard_map(
        on_device, mesh=mesh, in_specs=in_specs, out_specs=out_specs, check_vma=False
    )
```

profile of v0, /device:TPU:1, one launch (start us, length us, event | category | flops | bytes accessed | tf_op | source)
XLA Modules:
  0.0 352.5 jit_solution(10730294313552549575)
XLA Ops:
  6.5 0.7 compare_select_fusion.1
  7.2 0.7 compare_and_fusion.1
  7.9 1.0 slice_bitcast_fusion.1
  8.8 0.7 compare_bitcast_fusion.1
  10.2 8.1 %convert_bitcast_fusion.1 = bf16[64,256,256]{1,2,0:T(8,128)(2,1)} fusion(pred[64]{0:T(512)(128)(4,1)S(1)} %get-tuple-element.13, pred[64]{0:T(512)(128)(4,1)S(1)} %get-tuple-element.12, bf16[1,64,256,256]{3,2,1,0:T(8,128)(2,1)} %param.10, bf16[256,256]{1,0:T(8,128)(2,1)S(1)} %get-tuple-element.9, bf16[256,256]{1,0:T(8,128)(2,1)S(1)} %get-tuple-element.8, ...), kind=kOutput, calls=%fused_computation.10 | convolution fusion | flops 2164260864 | bytes 17039616 | tf_op jit(solution)/shard_map/kij,vkjl->vkil/dot_general | solution.py:25
  18.3 8.9 %gather_fusion = bf16[64,256,256]{1,2,0:T(8,128)(2,1)} fusion(bf16[64,256,256]{1,2,0:T(8,128)(2,1)} %convert_bitcast_fusion.1, s32[1024]{0:T(1024)S(1)} %pad_clamp_fusion.1), kind=kCustom, calls=%fused_computation.clone | custom fusion | bytes 16777472 | tf_op jit(solution)/shard_map/jit(_take)/gather | solution.py:28
  27.2 7.5 %fusion.2 = bf16[1,64,1,256,256]{3,4,2,0,1:T(8,128)(2,1)} fusion(bf16[64,256,256]{1,2,0:T(8,128)(2,1)} %gather_fusion, pred[64]{0:T(512)(128)(4,1)S(1)} %compare_and_fusion.1), kind=kLoop, calls=%fused_computation.6 | loop fusion | flops 4194304 | bytes 16777280 | tf_op jit(solution)/shard_map/reshape | solution.py:29
  34.7 0.0 copy-start.1
  34.7 0.0 copy-start.2
  34.7 0.0 copy-start
  34.7 13.5 %all-to-all-start = ((bf16[1,64,1,256,256]{3,4,2,0,1:T(8,128)(2,1)}), bf16[1,64,1,256,256]{3,4,2,0,1:T(8,128)(2,1)}, u32[]{:S(2)}, u32[]{:S(2)}) async-start(bf16[1,64,1,256,256]{3,4,2,0,1:T(8,128)(2,1)} %fusion.2), calls=%async_computation | async-start | bytes 16777216 | tf_op jit(solution)/shard_map/all_to_all | solution.py:30
  48.2 0.0 reduce-scatter.2.cloned.1.call-start
  48.2 0.0 copy-done.1
  48.3 0.0 copy-done.2
  48.3 0.0 copy-done
  48.3 185.6 %all-to-all-done = bf16[1,64,1,256,256]{3,4,2,0,1:T(8,128)(2,1)} async-done(((bf16[1,64,1,256,256]{3,4,2,0,1:T(8,128)(2,1)}), bf16[1,64,1,256,256]{3,4,2,0,1:T(8,128)(2,1)}, u32[]{:S(2)}, u32[]{:S(2)}) %all-to-all-start) | async-done | bytes 8388640 | tf_op jit(solution)/shard_map/all_to_all | solution.py:30
  233.9 8.9 %gather_fusion.1 = bf16[64,256,256]{1,2,0:T(8,128)(2,1)} fusion(bf16[64,256,256]{1,2,0:T(8,128)(2,1)} %bitcast.19, s32[1024]{0:T(1024)S(1)} %pad_clamp_fusion), kind=kCustom, calls=%fused_computation.1.clone | custom fusion | bytes 16777472 | tf_op jit(solution)/shard_map/jit(_take)/gather | solution.py:32
  242.8 6.9 %convert_bitcast_fusion = bf16[1,64,256,256]{2,3,1,0:T(8,128)(2,1)} fusion(bf16[64,256,256]{1,2,0:T(8,128)(2,1)} %gather_fusion.1, pred[64]{0:T(512)(128)(4,1)S(1)} %compare_and_fusion, pred[64]{0:T(512)(128)(4,1)S(1)} %get-tuple-element.11, pred[64]{0:T(512)(128)(4,1)S(1)} %get-tuple-element.10, bf16[256,256]{1,0:T(8,128)(2,1)S(1)} %get-tuple-element.7, ...), kind=kOutput, calls=%fused_computation.9 | convolution fusion | flops 2164260864 | bytes 17039552 | tf_op jit(solution)/shard_map/vkil,kml->vkim/dot_general | solution.py:34
  249.7 12.2 %copy.15 = bf16[1,64,256,256]{3,1,0,2:T(8,128)(2,1)} copy(bf16[1,64,256,256]{2,3,1,0:T(8,128)(2,1)} %convert_bitcast_fusion) | data formatting | bytes 16777216 | tf_op jit(solution)/shard_map/convert_element_type | solution.py:36
  261.9 0.0 reduce-scatter.2.cloned.1.call-update
  262.0 79.6 %reduce-scatter.2.cloned.1.call-done = bf16[1,64,64,256]{3,1,0,2:T(8,128)(2,1)} async-done(((bf16[1,64,256,256]{3,1,0,2:T(8,128)(2,1)}), bf16[1,64,64,256]{3,1,0,2:T(8,128)(2,1)}) %reduce-scatter.2.cloned.1.call-update) | async-done | bytes 2097168 | tf_op jit(solution)/shard_map/reduce_scatter | solution.py:37
  341.6 4.1 %copy.16 = bf16[1,64,64,256]{3,2,1,0:T(8,128)(2,1)} copy(bf16[1,64,64,256]{3,1,0,2:T(8,128)(2,1)} %reduce-scatter.2.cloned.1.call-done) | data formatting | bytes 4194304 | tf_op jit(solution)/shard_map/reduce_scatter | solution.py:37
  (7 shorter events, 0.1 us)
Async XLA Ops:
  34.7 13.5 %copy-start.1 = (s32[1,64]{1,0:T(1,128)S(1)}, s32[1,64]{1,0:T(1,128)}, u32[]{:S(2)}) copy-start(s32[1,64]{1,0:T(1,128)} %param.17) | copy-start | bytes 772
  34.7 13.6 %copy-start.2 = (s32[1,64]{1,0:T(1,128)S(1)}, s32[1,64]{1,0:T(1,128)}, u32[]{:S(2)}) copy-start(s32[1,64]{1,0:T(1,128)} %param.14) | copy-start | bytes 772
  34.7 13.6 %copy-start = (bf16[1,2,256,256]{3,2,1,0:T(8,128)(2,1)S(1)}, bf16[1,2,256,256]{3,2,1,0:T(8,128)(2,1)}, u32[]{:S(2)}) copy-start(bf16[1,2,256,256]{3,2,1,0:T(8,128)(2,1)} %param.12) | copy-start | bytes 786436
  34.7 199.2 %all-to-all-start = ((bf16[1,64,1,256,256]{3,4,2,0,1:T(8,128)(2,1)}), bf16[1,64,1,256,256]{3,4,2,0,1:T(8,128)(2,1)}, u32[]{:S(2)}, u32[]{:S(2)}) async-start(bf16[1,64,1,256,256]{3,4,2,0,1:T(8,128)(2,1)} %fusion.2), calls=%async_computation | async-start | bytes 16777216 | tf_op jit(solution)/shard_map/all_to_all | solution.py:30
  48.2 293.4 %reduce-scatter.2.cloned.1.call-start = ((), (), s32[]{:S(2)}) async-start(), calls=%async_computation.2 | async-start | bytes 10485760 | tf_op jit(solution)/shard_map/reduce_scatter | solution.py:37
Sparse Core Ops, SparseCore 0:
  262.1 79.4 reduce-scatter.1
where the time goes:
time: 353 us
  waiting for transfers between devices  265 us (75%)
  local copies, waits for them, and re-layouts  35.1 us (10%)
  matrix products  15 us (4%)
  between operations  14.1 us (4%)
  starting transfers between devices  13.5 us (4%)
  other arithmetic  9.5 us (3%)
    all_to_all x1, waiting for transfers between devices, on_device(): lax.all_to_all(outgoing, 'sec', split_axis=1, concat_axis=1, tiled=True)  186 us
    reduce_scatter x1, waiting for transfers between devices, on_device(): lax.psum_scatter(contrib.astype(jnp.float32).astype(jnp.bfloat16), 'term'...  79.6 us
    all_to_all x1, starting transfers between devices, on_device(): lax.all_to_all(outgoing, 'sec', split_axis=1, concat_axis=1, tiled=True)  13.5 us
    convert_element_type x1, local copies, waits for them, and re-layouts, on_device(): contrib = jnp.einsum('vkil,kml->vkim', placed, right_blocks, preferred_el...  12.2 us
    gather x1, local copies, waits for them, and re-layouts, on_device(): placed = jnp.take(incoming, arrival[0], axis=1)  8.92 us
    gather x1, local copies, waits for them, and re-layouts, on_device(): outgoing = jnp.take(applied, departure[0], axis=1)  8.92 us
    dot_general x1, matrix products, on_device(): jnp.einsum('kij,vkjl->vkil', left_blocks, masked, preferred_element_type=...  8.11 us
    reshape x1, other arithmetic, on_device(): outgoing = outgoing.reshape(n_vecs, n_sec, per_peer, width, width)  7.48 us
  transfers between devices with their start and end apart: 2, of which 2 were waited for; matrix products, arithmetic and copies ran while one was open for 0% of the time, Pallas kernels for 0%

commit v1 on v0

v1 whole, which is shorter than its diff:
```python
import functools

import jax
import jax.numpy as jnp
from jax import lax
from jax.experimental import pallas as pl
from jax.experimental.pallas import tpu as pltpu
from jax.sharding import PartitionSpec as P

CHUNK = 8
VMEM_LIMIT = 48 * 1024 * 1024


def _left_kernel(dep_ref, lsel_ref, live_ref, m_ref, x_ref, o_ref):
    base = pl.program_id(0) * CHUNK
    for k in range(CHUNK):
        e = base + k
        prod = jnp.dot(
            m_ref[lsel_ref[e]], x_ref[dep_ref[e]], preferred_element_type=jnp.float32
        )
        o_ref[k] = jnp.where(live_ref[e] > 0, prod, 0.0).astype(o_ref.dtype)


def apply_left(stacked, tiles, dep, lsel, live):
    n, w, _ = tiles.shape
    spec = pltpu.PrefetchScalarGridSpec(
        num_scalar_prefetch=3,
        grid=(n // CHUNK,),
        in_specs=[
            pl.BlockSpec(stacked.shape, lambda c, *_: (0, 0, 0)),
            pl.BlockSpec(tiles.shape, lambda c, *_: (0, 0, 0)),
        ],
        out_specs=pl.BlockSpec((CHUNK, w, w), lambda c, *_: (c, 0, 0)),
    )
    return pl.pallas_call(
        _left_kernel,
        grid_spec=spec,
        out_shape=jax.ShapeDtypeStruct((n, stacked.shape[1], w), jnp.bfloat16),
        compiler_params=pltpu.CompilerParams(vmem_limit_bytes=VMEM_LIMIT),
        cost_estimate=pl.CostEstimate(
            flops=2 * n * stacked.shape[1] * w * w,
            bytes_accessed=2 * (2 * n * w * w + stacked.size),
            transcendentals=0,
        ),
    )(dep, lsel, live, stacked, tiles)


def _right_kernel(n_term, arr_ref, rsel_ref, a_ref, r_ref, o_ref):
    base = pl.program_id(0) * CHUNK
    rows = o_ref.shape[1]
    for k in range(CHUNK):
        s = base + k
        block = a_ref[arr_ref[s]]
        sector = rsel_ref[s]
        acc = None
        for tp in range(n_term):
            part = lax.dot_general(
                block[tp * rows:(tp + 1) * rows],
                r_ref[tp * 2 + sector],
                (((1,), (1,)), ((), ())),
                preferred_element_type=jnp.float32,
            )
            acc = part if acc is None else acc + part
        o_ref[k] = acc.astype(o_ref.dtype)


def apply_right(placed, right_all, arr, rsel, n_term):
    n, height, w = placed.shape
    rows = height // n_term
    spec = pltpu.PrefetchScalarGridSpec(
        num_scalar_prefetch=2,
        grid=(n // CHUNK,),
        in_specs=[
            pl.BlockSpec(placed.shape, lambda c, *_: (0, 0, 0)),
            pl.BlockSpec(right_all.shape, lambda c, *_: (0, 0, 0)),
        ],
        out_specs=pl.BlockSpec((CHUNK, rows, w), lambda c, *_: (c, 0, 0)),
    )
    return pl.pallas_call(
        functools.partial(_right_kernel, n_term),
        grid_spec=spec,
        out_shape=jax.ShapeDtypeStruct((n, rows, w), jnp.bfloat16),
        compiler_params=pltpu.CompilerParams(vmem_limit_bytes=VMEM_LIMIT),
        cost_estimate=pl.CostEstimate(
            flops=2 * n * height * w * w,
            bytes_accessed=2 * (n * height * w + right_all.size + n * rows * w),
            transcendentals=0,
        ),
    )(arr, rsel, placed, right_all)


def on_device(
    vectors, left_env, right_env, left_sector, right_sector, tile_count, departure, arrival
):
    n_term = lax.axis_size("term")
    n_vecs, tiles_dev, width, _ = vectors.shape
    n_sec_local = left_env.shape[1]
    rows = width // n_term

    left_rows = lax.all_to_all(
        left_env[0].reshape(n_sec_local, n_term, rows, width),
        "term", split_axis=1, concat_axis=1, tiled=True,
    )
    stacked = left_rows.reshape(n_sec_local, n_term * rows, width)

    right_all = lax.all_to_all(
        jnp.broadcast_to(right_env, (n_term,) + right_env.shape[1:]),
        "term", split_axis=0, concat_axis=0, tiled=True,
    ).reshape(n_term * n_sec_local, width, width)

    dep = departure[0]
    lsel = jnp.take(left_sector[0], dep)
    live = (dep < tile_count[0]).astype(jnp.int32)
    arr = arrival[0]
    rsel = right_sector[0]

    outs = []
    for v in range(n_vecs):
        outgoing = apply_left(stacked, vectors[v], dep, lsel, live)
        incoming = lax.all_to_all(outgoing, "sec", split_axis=0, concat_axis=0, tiled=True)
        outs.append(apply_right(incoming, right_all, arr, rsel, n_term))
    return jnp.stack(outs)


def solution(mesh):
    in_specs = (
        P(None, "sec", None, None),
        P("term", "sec", None, None),
        P("term", "sec", None, None),
        P("sec", None),
        P("sec", None),
        P("sec"),
        P("sec", None),
        P("sec", None),
    )
    out_specs = P(None, "sec", "term", None)
    return jax.shard_map(
        on_device, mesh=mesh, in_specs=in_specs, out_specs=out_specs, check_vma=False
    )
```

time: 353 us -> 247 us (0.70)
  waiting for transfers between devices: 265 us -> 0.01 us
  blocking collectives: 0 us -> 210 us
  local copies, waits for them, and re-layouts: 35.1 us -> 4.42 us
  Pallas kernels: 0 us -> 26 us
  matrix products: 15 us -> 0 us
  between operations: 14.1 us -> 0.7 us
  starting transfers between devices: 13.5 us -> 3.52 us
  other arithmetic: 9.5 us -> 1.99 us
    all_to_all x0 -> x2, blocking collectives: none -> 210 us  [the longest x1 200 us: on_device(): lax.all_to_all(outgoing, 'sec', split_axis=0, concat_axis=0, tiled=True)]
    all_to_all x1, waiting for transfers between devices: 186 us -> 0.01 us  [on_device(): lax.all_to_all(jnp.broadcast_to(right_env, (n_term,) + right_env.shape[1:...]
    reduce_scatter x1 -> x0, waiting for transfers between devices: 79.6 us -> none  [on_device(): lax.psum_scatter(contrib.astype(jnp.float32).astype(jnp.bfloat16), 'term'...]
    pallas_call x0 -> x2, Pallas kernels: none -> 26 us  [the longest x1 15.8 us: apply_right(): pl.pallas_call(functools.partial(_right_kernel, n_term), grid_spec=spec,...]
    gather x2 -> x1, local copies, waits for them, and re-layouts: 17.8 us -> 0.77 us  [on_device(): lsel = jnp.take(left_sector[0], dep)]
    dot_general x2 -> x0, matrix products: 15 us -> none  [the longest x1 8.11 us: on_device(): jnp.einsum('kij,vkjl->vkil', left_blocks, masked, preferred_element_type=...]
    convert_element_type x1 -> x0, local copies, waits for them, and re-layouts: 12.2 us -> none  [on_device(): contrib = jnp.einsum('vkil,kml->vkim', placed, right_blocks, preferred_el...]
    all_to_all x1, starting transfers between devices: 13.5 us -> 3.52 us  [on_device(): lax.all_to_all(jnp.broadcast_to(right_env, (n_term,) + right_env.shape[1:...]
  transfers between devices with their start and end apart: 2 -> 1, of which waited for: 2 -> 0; matrix products, arithmetic and copies ran while one was open for 0% -> 1% of each run, Pallas kernels for 0% -> 4%
where the time goes in v1:
time: 247 us
  blocking collectives  210 us (85%)
  Pallas kernels  26 us (11%)
  local copies, waits for them, and re-layouts  4.42 us (2%)
  starting transfers between devices  3.52 us (1%)
    all_to_all x1, blocking collectives, on_device(): lax.all_to_all(outgoing, 'sec', split_axis=0, concat_axis=0, tiled=True)  200 us
    pallas_call x1, Pallas kernels, apply_right(): pl.pallas_call(functools.partial(_right_kernel, n_term), grid_spec=spec,...  15.8 us
    pallas_call x1, Pallas kernels, apply_left(): pl.pallas_call(_left_kernel, grid_spec=spec, out_shape=jax.ShapeDtypeStru...  10.3 us
    all_to_all x1, blocking collectives, on_device(): lax.all_to_all(left_env[0].reshape(n_sec_local, n_term, rows, width), 'te...  10.2 us
  transfers between devices with their start and end apart: 1, of which 0 were waited for; matrix products, arithmetic and copies ran while one was open for 1% of the time, Pallas kernels for 4%

profile of v1, /device:TPU:1, one launch (start us, length us, event | category | flops | bytes accessed | tf_op | source)
XLA Modules:
  0.0 246.8 jit_solution(17022221498398509925)
XLA Ops:
  0.0 0.0 copy-start
  0.0 1.0 copy.10
  1.0 10.2 %all_to_all.15 = bf16[2,4,64,256]{3,2,0,1:T(8,128)(2,1)S(1)} all-to-all(bf16[2,4,64,256]{3,2,0,1:T(8,128)(2,1)S(1)} %copy.10), channel_id=1, replica_groups=mesh['term'=4,'sec'=64] {'term'}, dimensions={1} | all-to-all | bytes 524288 | tf_op jit(solution)/shard_map/all_to_all | solution.py:100
  11.2 2.0 broadcast_in_dim.15
  13.2 3.5 %all-to-all-start.2 = ((bf16[4,2,256,256]{3,2,1,0:T(8,128)(2,1)}), bf16[4,2,256,256]{3,2,1,0:T(8,128)(2,1)S(1)}, u32[]{:S(2)}, u32[]{:S(2)}) async-start(bf16[4,2,256,256]{3,2,1,0:T(8,128)(2,1)} %broadcast_in_dim.15), calls=%async_computation.2 | async-start | bytes 2097152 | tf_op jit(solution)/shard_map/all_to_all | solution.py:106
  16.7 0.7 fusion
  18.0 0.0 copy-done
  18.0 0.8 gather_fusion
  18.8 0.7 compare_convert_fusion.live_ref
  19.5 0.7 and_select_fusion.lsel_ref
  20.1 0.0 copy-start.1
  20.2 0.6 copy-done.1
  20.8 10.3 %shard_map.82 = bf16[64,256,256]{2,1,0:T(8,128)(2,1)} custom-call(s32[64]{0:T(128)S(1)} %bitcast.21, s32[64]{0:T(128)S(1)} %and_select_fusion.lsel_ref, s32[64]{0:T(128)S(1)} %compare_convert_fusion.live_ref, bf16[2,256,256]{2,1,0:T(8,128)(2,1)S(1)} %bitcast.20, bf16[64,256,256]{2,1,0:T(8,128)(2,1)} %bitcast.24), custom_call_target="tpu_custom_call" | custom-call | flops 2147483648 | bytes 17039360 | tf_op jit(solution)/shard_map/pallas_call | solution.py:35
  31.1 0.0 copy-start.2
  31.1 0.0 copy-start.3
  31.1 0.0 all-to-all-done.2
  31.1 200.0 %all_to_all.16.a_ref = bf16[64,256,256]{2,1,0:T(8,128)(2,1)} all-to-all(bf16[64,256,256]{2,1,0:T(8,128)(2,1)} %shard_map.82), channel_id=1, replica_groups=mesh['term'=4,'sec'=64] {'sec'}, dimensions={0} | all-to-all | bytes 16777216 | tf_op jit(solution)/shard_map/all_to_all | solution.py:120
  231.1 0.0 copy-done.2
  231.1 0.0 copy-done.3
  231.1 15.8 %shard_map.83 = bf16[64,64,256]{2,1,0:T(8,128)(2,1)} custom-call(s32[64]{0:T(128)S(1)} %bitcast.22, s32[64]{0:T(128)S(1)} %bitcast.23, bf16[64,256,256]{2,1,0:T(8,128)(2,1)} %all_to_all.16.a_ref, bf16[8,256,256]{2,1,0:T(8,128)(2,1)S(1)} %bitcast.19), custom_call_target="tpu_custom_call" | custom-call | flops 2147483648 | bytes 11534336 | tf_op jit(solution)/shard_map/pallas_call | solution.py:79
  (2 shorter events, 0.0 us)
Async XLA Ops:
  0.0 18.0 %copy-start = (s32[1,64]{1,0:T(1,128)S(1)}, s32[1,64]{1,0:T(1,128)}, u32[]{:S(2)}) copy-start(s32[1,64]{1,0:T(1,128)} %param.11) | copy-start | bytes 772
  13.2 17.9 %all-to-all-start.2 = ((bf16[4,2,256,256]{3,2,1,0:T(8,128)(2,1)}), bf16[4,2,256,256]{3,2,1,0:T(8,128)(2,1)S(1)}, u32[]{:S(2)}, u32[]{:S(2)}) async-start(bf16[4,2,256,256]{3,2,1,0:T(8,128)(2,1)} %broadcast_in_dim.15), calls=%async_computation.2 | async-start | bytes 2097152 | tf_op jit(solution)/shard_map/all_to_all | solution.py:106
  20.1 0.7 copy-start.1
  31.1 200.0 %copy-start.2 = (s32[1,64]{1,0:T(1,128)S(1)}, s32[1,64]{1,0:T(1,128)}, u32[]{:S(2)}) copy-start(s32[1,64]{1,0:T(1,128)} %param.15) | copy-start | bytes 772
  31.1 200.0 %copy-start.3 = (s32[1,64]{1,0:T(1,128)S(1)}, s32[1,64]{1,0:T(1,128)}, u32[]{:S(2)}) copy-start(s32[1,64]{1,0:T(1,128)} %param.12) | copy-start | bytes 772

commit v2 on v1

v2 whole, which is shorter than its diff:
```python
import functools

import jax
import jax.numpy as jnp
from jax import lax
from jax.experimental import pallas as pl
from jax.experimental.pallas import tpu as pltpu
from jax.sharding import PartitionSpec as P

CHUNK = 8
VMEM_LIMIT = 48 * 1024 * 1024


def _left_kernel(dep_ref, lsel_ref, live_ref, idx_ref, l_ref, x_ref, o_ref):
    base = pl.program_id(0) * CHUNK
    for k in range(CHUNK):
        e = base + k
        prod = jnp.dot(
            l_ref[lsel_ref[e], 0], x_ref[dep_ref[e]], preferred_element_type=jnp.float32
        )
        o_ref[k] = jnp.where(live_ref[e] > 0, prod, 0.0).astype(o_ref.dtype)


def apply_left(slabs, tiles, dep, lsel, live, idx):
    n, w, _ = tiles.shape
    n_sector, _, rows, _ = slabs.shape
    spec = pltpu.PrefetchScalarGridSpec(
        num_scalar_prefetch=4,
        grid=(n // CHUNK,),
        in_specs=[
            pl.BlockSpec((n_sector, 1, rows, w), lambda c, d, s, v, i: (0, i[0], 0, 0)),
            pl.BlockSpec(tiles.shape, lambda c, *_: (0, 0, 0)),
        ],
        out_specs=pl.BlockSpec((CHUNK, rows, w), lambda c, *_: (c, 0, 0)),
    )
    return pl.pallas_call(
        _left_kernel,
        grid_spec=spec,
        out_shape=jax.ShapeDtypeStruct((n, rows, w), jnp.bfloat16),
        compiler_params=pltpu.CompilerParams(vmem_limit_bytes=VMEM_LIMIT),
        cost_estimate=pl.CostEstimate(
            flops=2 * n * rows * w * w,
            bytes_accessed=2 * (n * w * w + n * rows * w),
            transcendentals=0,
        ),
    )(dep, lsel, live, idx, slabs, tiles)


def _right_kernel(accumulate, arr_ref, rsel_ref, idx_ref, a_ref, r_ref, *rest):
    if accumulate:
        acc_ref, o_ref = rest
    else:
        (o_ref,) = rest
    base = pl.program_id(0) * CHUNK
    for k in range(CHUNK):
        s = base + k
        part = lax.dot_general(
            a_ref[arr_ref[s]],
            r_ref[0, rsel_ref[s]],
            (((1,), (1,)), ((), ())),
            preferred_element_type=jnp.float32,
        )
        if accumulate:
            part = part + acc_ref[k]
        o_ref[k] = part.astype(o_ref.dtype)


def apply_right(placed, blocks, arr, rsel, idx, acc, out_dtype):
    n, rows, w = placed.shape
    n_sector = blocks.shape[1]
    in_specs = [
        pl.BlockSpec(placed.shape, lambda c, *_: (0, 0, 0)),
        pl.BlockSpec((1, n_sector, w, w), lambda c, a, r, i: (i[0], 0, 0, 0)),
    ]
    operands = [arr, rsel, idx, placed, blocks]
    aliases = {}
    if acc is not None:
        in_specs.append(pl.BlockSpec((CHUNK, rows, w), lambda c, *_: (c, 0, 0)))
        operands.append(acc)
        if acc.dtype == out_dtype:
            aliases = {5: 0}
    spec = pltpu.PrefetchScalarGridSpec(
        num_scalar_prefetch=3,
        grid=(n // CHUNK,),
        in_specs=in_specs,
        out_specs=pl.BlockSpec((CHUNK, rows, w), lambda c, *_: (c, 0, 0)),
    )
    return pl.pallas_call(
        functools.partial(_right_kernel, acc is not None),
        grid_spec=spec,
        out_shape=jax.ShapeDtypeStruct((n, rows, w), out_dtype),
        input_output_aliases=aliases,
        compiler_params=pltpu.CompilerParams(vmem_limit_bytes=VMEM_LIMIT),
        cost_estimate=pl.CostEstimate(
            flops=2 * n * rows * w * w,
            bytes_accessed=2 * n * rows * w + 2 * n_sector * w * w + 8 * n * rows * w,
            transcendentals=0,
        ),
    )(*operands)


def on_device(
    vectors, left_env, right_env, left_sector, right_sector, tile_count, departure, arrival
):
    n_term = lax.axis_size("term")
    me = lax.axis_index("term")
    n_vecs, tiles_dev, width, _ = vectors.shape
    n_sector = left_env.shape[1]
    rows = width // n_term

    own_left = left_env[0].reshape(n_sector, n_term, rows, width)
    left_rows = lax.all_to_all(own_left, "term", split_axis=1, concat_axis=1, tiled=True)
    right_all = lax.all_to_all(
        jnp.broadcast_to(right_env, (n_term,) + right_env.shape[1:]),
        "term", split_axis=0, concat_axis=0, tiled=True,
    )

    dep = departure[0]
    lsel = jnp.take(left_sector[0], dep)
    live = (dep < tile_count[0]).astype(jnp.int32)
    arr = arrival[0]
    rsel = right_sector[0]

    outs = []
    for v in range(n_vecs):
        acc = None
        for c in range(n_term):
            term = (me + c) % n_term
            if c == 0:
                slabs, lidx = own_left, me
                blocks, ridx = right_env, jnp.int32(0)
            else:
                slabs, lidx = left_rows, term
                blocks, ridx = right_all, term
            lidx = jnp.reshape(lidx, (1,)).astype(jnp.int32)
            ridx = jnp.reshape(ridx, (1,)).astype(jnp.int32)
            outgoing = apply_left(slabs, vectors[v], dep, lsel, live, lidx)
            incoming = lax.all_to_all(outgoing, "sec", split_axis=0, concat_axis=0, tiled=True)
            last = c == n_term - 1
            acc = apply_right(
                incoming, blocks, arr, rsel, ridx, acc,
                vectors.dtype if last else jnp.float32,
            )
        outs.append(acc)
    return jnp.stack(outs)


def solution(mesh):
    in_specs = (
        P(None, "sec", None, None),
        P("term", "sec", None, None),
        P("term", "sec", None, None),
        P("sec", None),
        P("sec", None),
        P("sec"),
        P("sec", None),
        P("sec", None),
    )
    out_specs = P(None, "sec", "term", None)
    return jax.shard_map(
        on_device, mesh=mesh, in_specs=in_specs, out_specs=out_specs, check_vma=False
    )
```

time: 247 us -> 280 us (1.13)
  blocking collectives: 210 us -> 0 us
  waiting for transfers between devices: 0.01 us -> 163 us
  starting transfers between devices: 3.52 us -> 41.9 us
  Pallas kernels: 26 us -> 58.1 us
  local copies, waits for them, and re-layouts: 4.42 us -> 15.1 us
    all_to_all x2 -> x0, blocking collectives: 210 us -> none  [the longest x1 200 us: on_device(): lax.all_to_all(outgoing, 'sec', split_axis=0, concat_axis=0, tiled=True)]
    all_to_all x0 -> x5, waiting for transfers between devices: none -> 160 us  [the longest x4 155 us: on_device(): lax.all_to_all(outgoing, 'sec', split_axis=0, concat_axis=0, tiled=True)]
    all_to_all x0 -> x5, starting transfers between devices: none -> 38.4 us  [the longest x4 33.4 us: on_device(): lax.all_to_all(outgoing, 'sec', split_axis=0, concat_axis=0, tiled=True)]
    pallas_call x1 -> x4, Pallas kernels: 15.8 us -> 32.1 us  [apply_right(): pl.pallas_call(functools.partial(_right_kernel, acc is not None), grid_sp...]
    pallas_call x1 -> x4, Pallas kernels: 10.3 us -> 26 us  [apply_left(): pl.pallas_call(_left_kernel, grid_spec=spec, out_shape=jax.ShapeDtypeStru...]
    unnamed x8 -> x30, local copies, waits for them, and re-layouts: 0.66 us -> 9.58 us
    all_to_all x1, waiting for transfers between devices: 0.01 us -> 3.28 us  [on_device(): lax.all_to_all(jnp.broadcast_to(right_env, (n_term,) + right_env.shape[1:...]
  transfers between devices with their start and end apart: 1 -> 6, of which waited for: 0 -> 6; matrix products, arithmetic and copies ran while one was open for 1% -> 1% of each run, Pallas kernels for 4% -> 18%
where the time goes in v2:
time: 280 us; the launch traced here: 279 us
  waiting for transfers between devices  163 us (58%)
  Pallas kernels  58.1 us (21%)
  starting transfers between devices  41.9 us (15%)
  local copies, waits for them, and re-layouts  15.1 us (5%)
    all_to_all x4, waiting for transfers between devices, on_device(): lax.all_to_all(outgoing, 'sec', split_axis=0, concat_axis=0, tiled=True)  155 us
    all_to_all x4, starting transfers between devices, on_device(): lax.all_to_all(outgoing, 'sec', split_axis=0, concat_axis=0, tiled=True)  33.4 us
    pallas_call x4, Pallas kernels, apply_right(): pl.pallas_call(functools.partial(_right_kernel, acc is not None), grid_sp...  32.1 us
    pallas_call x4, Pallas kernels, apply_left(): pl.pallas_call(_left_kernel, grid_spec=spec, out_shape=jax.ShapeDtypeStru...  26 us
    unnamed x30, local copies, waits for them, and re-layouts  9.58 us
  transfers between devices with their start and end apart: 6, of which 6 were waited for; matrix products, arithmetic and copies ran while one was open for 1% of the time, Pallas kernels for 18%

profile of v2, /device:TPU:1, one launch (start us, length us, event | category | flops | bytes accessed | tf_op | source)
XLA Modules:
  0.0 278.9 jit_solution(16285881749813977164)
XLA Ops:
  0.0 1.7 copy.11
  1.7 5.0 %all-to-all-start = ((bf16[2,4,64,256]{3,2,0,1:T(8,128)(2,1)}), bf16[2,4,64,256]{3,2,0,1:T(8,128)(2,1)S(1)}, u32[]{:S(2)}, u32[]{:S(2)}) async-start(bf16[2,4,64,256]{3,2,0,1:T(8,128)(2,1)} %copy.11), calls=%async_computation | async-start | bytes 524288 | tf_op jit(solution)/shard_map/all_to_all | solution.py:112
  7.3 4.8 %all-to-all-done = bf16[2,4,64,256]{3,2,0,1:T(8,128)(2,1)S(1)} async-done(((bf16[2,4,64,256]{3,2,0,1:T(8,128)(2,1)}), bf16[2,4,64,256]{3,2,0,1:T(8,128)(2,1)S(1)}, u32[]{:S(2)}, u32[]{:S(2)}) %all-to-all-start) | async-done | bytes 262176 | tf_op jit(solution)/shard_map/all_to_all | solution.py:112
  12.2 2.1 broadcast_in_dim.15
  14.3 3.5 %all-to-all-start.2 = ((bf16[4,2,256,256]{3,2,1,0:T(8,128)(2,1)}), bf16[4,2,256,256]{3,2,1,0:T(8,128)(2,1)S(1)}, u32[]{:S(2)}, u32[]{:S(2)}) async-start(bf16[4,2,256,256]{3,2,1,0:T(8,128)(2,1)} %broadcast_in_dim.15), calls=%async_computation.2 | async-start | bytes 2097152 | tf_op jit(solution)/shard_map/all_to_all | solution.py:113
  17.8 0.8 gather_fusion
  18.6 6.5 %shard_map.85 = bf16[64,64,256]{2,1,0:T(8,128)(2,1)S(1)} custom-call(s32[64]{0:T(128)S(1)} %bitcast.24, s32[64]{0:T(128)S(1)} %and_select_fusion.lsel_ref, s32[64]{0:T(128)S(1)} %compare_convert_fusion.live_ref, s32[1]{0:T(128)} %bitcast.13.idx_ref, bf16[2,4,64,256]{3,2,1,0:T(8,128)(2,1)S(1)} %bitcast.23, bf16[64,256,256]{2,1,0:T(8,128)(2,1)} %bitcast.36), custom_call_target="tpu_custom_call" | custom-call | flops 536870912 | bytes 10485760 | tf_op jit(solution)/shard_map/pallas_call | solution.py:36
  25.2 1.3 copy-done.6
  26.5 3.3 %all-to-all-done.2.r_ref = bf16[4,2,256,256]{3,2,1,0:T(8,128)(2,1)S(1)} async-done(((bf16[4,2,256,256]{3,2,1,0:T(8,128)(2,1)}), bf16[4,2,256,256]{3,2,1,0:T(8,128)(2,1)S(1)}, u32[]{:S(2)}, u32[]{:S(2)}) %all-to-all-start.2) | async-done | bytes 1048608 | tf_op jit(solution)/shard_map/all_to_all | solution.py:113
  29.8 15.7 %all-to-all-start.5 = ((bf16[64,64,256]{2,1,0:T(8,128)(2,1)}), bf16[64,64,256]{2,1,0:T(8,128)(2,1)S(1)}, u32[]{:S(2)}, u32[]{:S(2)}) async-start(bf16[64,64,256]{2,1,0:T(8,128)(2,1)} %copy-done.6), calls=%async_computation.5 | async-start | bytes 4194304 | tf_op jit(solution)/shard_map/all_to_all | solution.py:138
  45.5 1.0 copy.12.l_ref
  46.5 6.5 %shard_map.84 = bf16[64,64,256]{2,1,0:T(8,128)(2,1)S(1)} custom-call(s32[64]{0:T(128)S(1)} %bitcast.25, s32[64]{0:T(128)S(1)} %and_select_fusion.lsel_ref, s32[64]{0:T(128)S(1)} %compare_convert_fusion.live_ref, s32[1]{0:T(128)} %bitcast.12.idx_ref, bf16[2,4,64,256]{3,2,1,0:T(8,128)(2,1)S(1)} %copy.12.l_ref, bf16[64,256,256]{2,1,0:T(8,128)(2,1)} %bitcast.37), custom_call_target="tpu_custom_call" | custom-call | flops 536870912 | bytes 10485760 | tf_op jit(solution)/shard_map/pallas_call | solution.py:36
  53.0 0.0 copy-start.7
  53.0 1.3 copy-done.7
  54.3 42.4 %all-to-all-done.5.a_ref = bf16[64,64,256]{2,1,0:T(8,128)(2,1)S(1)} async-done(((bf16[64,64,256]{2,1,0:T(8,128)(2,1)}), bf16[64,64,256]{2,1,0:T(8,128)(2,1)S(1)}, u32[]{:S(2)}, u32[]{:S(2)}) %all-to-all-start.5) | async-done | bytes 2097184 | tf_op jit(solution)/shard_map/all_to_all | solution.py:138
  96.7 1.3 copy-done.1
  98.0 6.0 %all-to-all-start.4 = ((bf16[64,64,256]{2,1,0:T(8,128)(2,1)}), bf16[64,64,256]{2,1,0:T(8,128)(2,1)}, u32[]{:S(2)}, u32[]{:S(2)}) async-start(bf16[64,64,256]{2,1,0:T(8,128)(2,1)} %copy-done.7), calls=%async_computation.4 | async-start | bytes 4194304 | tf_op jit(solution)/shard_map/all_to_all | solution.py:138
  104.1 6.5 %shard_map.83 = bf16[64,64,256]{2,1,0:T(8,128)(2,1)S(1)} custom-call(s32[64]{0:T(128)S(1)} %bitcast.26, s32[64]{0:T(128)S(1)} %and_select_fusion.lsel_ref, s32[64]{0:T(128)S(1)} %compare_convert_fusion.live_ref, s32[1]{0:T(128)} %bitcast.11.idx_ref, bf16[2,4,64,256]{3,2,1,0:T(8,128)(2,1)S(1)} %copy.12.l_ref, bf16[64,256,256]{2,1,0:T(8,128)(2,1)} %bitcast.38), custom_call_target="tpu_custom_call" | custom-call | flops 536870912 | bytes 10485760 | tf_op jit(solution)/shard_map/pallas_call | solution.py:36
  110.6 1.3 copy-done.5
  111.9 43.3 %all-to-all-done.4.a_ref = bf16[64,64,256]{2,1,0:T(8,128)(2,1)} async-done(((bf16[64,64,256]{2,1,0:T(8,128)(2,1)}), bf16[64,64,256]{2,1,0:T(8,128)(2,1)}, u32[]{:S(2)}, u32[]{:S(2)}) %all-to-all-start.4) | async-done | bytes 2097184 | tf_op jit(solution)/shard_map/all_to_all | solution.py:138
  155.2 5.8 %all-to-all-start.3 = ((bf16[64,64,256]{2,1,0:T(8,128)(2,1)}), bf16[64,64,256]{2,1,0:T(8,128)(2,1)S(1)}, u32[]{:S(2)}, u32[]{:S(2)}) async-start(bf16[64,64,256]{2,1,0:T(8,128)(2,1)} %copy-done.5), calls=%async_computation.3 | async-start | bytes 4194304 | tf_op jit(solution)/shard_map/all_to_all | solution.py:138
  161.0 6.5 %shard_map.82 = bf16[64,64,256]{2,1,0:T(8,128)(2,1)S(1)} custom-call(s32[64]{0:T(128)S(1)} %bitcast.27, s32[64]{0:T(128)S(1)} %and_select_fusion.lsel_ref, s32[64]{0:T(128)S(1)} %compare_convert_fusion.live_ref, s32[1]{0:T(128)} %bitcast.2.idx_ref, bf16[2,4,64,256]{3,2,1,0:T(8,128)(2,1)S(1)} %copy.12.l_ref, bf16[64,256,256]{2,1,0:T(8,128)(2,1)} %bitcast.39), custom_call_target="tpu_custom_call" | custom-call | flops 536870912 | bytes 10485760 | tf_op jit(solution)/shard_map/pallas_call | solution.py:36
  167.5 1.3 copy-done.8
  168.9 43.4 %all-to-all-done.3.a_ref = bf16[64,64,256]{2,1,0:T(8,128)(2,1)S(1)} async-done(((bf16[64,64,256]{2,1,0:T(8,128)(2,1)}), bf16[64,64,256]{2,1,0:T(8,128)(2,1)S(1)}, u32[]{:S(2)}, u32[]{:S(2)}) %all-to-all-start.3) | async-done | bytes 2097184 | tf_op jit(solution)/shard_map/all_to_all | solution.py:138
  212.2 1.4 copy-done.3
  213.6 5.8 %all-to-all-start.1 = ((bf16[64,64,256]{2,1,0:T(8,128)(2,1)}), bf16[64,64,256]{2,1,0:T(8,128)(2,1)S(1)}, u32[]{:S(2)}, u32[]{:S(2)}) async-start(bf16[64,64,256]{2,1,0:T(8,128)(2,1)} %copy-done.8), calls=%async_computation.1 | async-start | bytes 4194304 | tf_op jit(solution)/shard_map/all_to_all | solution.py:138
  219.5 1.6 copy-done.2
  221.1 6.0 %shard_map.86.rest_0_ = f32[64,64,256]{2,1,0:T(8,128)} custom-call(s32[64]{0:T(128)S(1)} %bitcast.28, s32[64]{0:T(128)S(1)} %bitcast.32, s32[1]{0:T(128)} %constant.48.clone.1.idx_ref, bf16[64,64,256]{2,1,0:T(8,128)(2,1)S(1)} %copy-done.2, bf16[1,2,256,256]{3,2,1,0:T(8,128)(2,1)S(1)} %copy-done.9), custom_call_target="tpu_custom_call" | custom-call | flops 536870912 | bytes 10747904 | tf_op jit(solution)/shard_map/pallas_call | solution.py:88
  227.1 9.4 %shard_map.87.rest_0_ = f32[64,64,256]{2,1,0:T(8,128)} custom-call(s32[64]{0:T(128)S(1)} %bitcast.29, s32[64]{0:T(128)S(1)} %bitcast.33, s32[1]{0:T(128)} %bitcast.12.idx_ref, bf16[64,64,256]{2,1,0:T(8,128)(2,1)} %all-to-all-done.4.a_ref, bf16[4,2,256,256]{3,2,1,0:T(8,128)(2,1)S(1)} %all-to-all-done.2.r_ref, ...), custom_call_target="tpu_custom_call", output_to_operand_aliasing={{}: (5, {})} | custom-call | flops 536870912 | bytes 10747904 | tf_op jit(solution)/shard_map/pallas_call | solution.py:88
  236.4 8.6 %shard_map.88.rest_0_ = f32[64,64,256]{2,1,0:T(8,128)} custom-call(s32[64]{0:T(128)S(1)} %bitcast.30, s32[64]{0:T(128)S(1)} %bitcast.34, s32[1]{0:T(128)} %bitcast.11.idx_ref, bf16[64,64,256]{2,1,0:T(8,128)(2,1)S(1)} %copy-done.4, bf16[4,2,256,256]{3,2,1,0:T(8,128)(2,1)S(1)} %all-to-all-done.2.r_ref, ...), custom_call_target="tpu_custom_call", output_to_operand_aliasing={{}: (5, {})} | custom-call | flops 536870912 | bytes 10747904 | tf_op jit(solution)/shard_map/pallas_call | solution.py:88
  245.0 25.7 %all-to-all-done.1.a_ref = bf16[64,64,256]{2,1,0:T(8,128)(2,1)S(1)} async-done(((bf16[64,64,256]{2,1,0:T(8,128)(2,1)}), bf16[64,64,256]{2,1,0:T(8,128)(2,1)S(1)}, u32[]{:S(2)}, u32[]{:S(2)}) %all-to-all-start.1) | async-done | bytes 2097184 | tf_op jit(solution)/shard_map/all_to_all | solution.py:138
  270.7 8.2 %shard_map.89 = bf16[64,64,256]{2,1,0:T(8,128)(2,1)} custom-call(s32[64]{0:T(128)S(1)} %bitcast.31, s32[64]{0:T(128)S(1)} %bitcast.35, s32[1]{0:T(128)} %bitcast.2.idx_ref, bf16[64,64,256]{2,1,0:T(8,128)(2,1)S(1)} %all-to-all-done.1.a_ref, bf16[4,2,256,256]{3,2,1,0:T(8,128)(2,1)S(1)} %all-to-all-done.2.r_ref, f32[64,64,256]{2,1,0:T(8,128)} %shard_map.88.rest_0_), custom_call_target="tpu_custom_call" | custom-call | flops 536870912 | bytes 10747904 | tf_op jit(solution)/shard_map/pallas_call | solution.py:88
  (26 shorter events, 0.1 us)
Async XLA Ops:
  0.0 17.8 %copy-start = (s32[1,64]{1,0:T(1,128)S(1)}, s32[1,64]{1,0:T(1,128)}, u32[]{:S(2)}) copy-start(s32[1,64]{1,0:T(1,128)} %param.11) | copy-start | bytes 772
  1.7 16.1 %copy-start.11 = (s32[1,64]{1,0:T(1,128)S(1)}, s32[1,64]{1,0:T(1,128)}, u32[]{:S(2)}) copy-start(s32[1,64]{1,0:T(1,128)} %param.14) | copy-start | bytes 772
  1.7 10.5 %all-to-all-start = ((bf16[2,4,64,256]{3,2,0,1:T(8,128)(2,1)}), bf16[2,4,64,256]{3,2,0,1:T(8,128)(2,1)S(1)}, u32[]{:S(2)}, u32[]{:S(2)}) async-start(bf16[2,4,64,256]{3,2,0,1:T(8,128)(2,1)} %copy.11), calls=%async_computation | async-start | bytes 524288 | tf_op jit(solution)/shard_map/all_to_all | solution.py:112
  6.7 12.0 %copy-start.10 = (bf16[1,2,256,256]{3,2,1,0:T(8,128)(2,1)S(1)}, bf16[1,2,256,256]{3,2,1,0:T(8,128)(2,1)}, u32[]{:S(2)}) copy-start(bf16[1,2,256,256]{3,2,1,0:T(8,128)(2,1)} %param.9) | copy-start | bytes 786436
  12.2 2.1 copy-start.14
  14.3 15.5 %all-to-all-start.2 = ((bf16[4,2,256,256]{3,2,1,0:T(8,128)(2,1)}), bf16[4,2,256,256]{3,2,1,0:T(8,128)(2,1)S(1)}, u32[]{:S(2)}, u32[]{:S(2)}) async-start(bf16[4,2,256,256]{3,2,1,0:T(8,128)(2,1)} %broadcast_in_dim.15), calls=%async_computation.2 | async-start | bytes 2097152 | tf_op jit(solution)/shard_map/all_to_all | solution.py:113
  25.1 1.3 copy-start.6
  29.8 66.9 %all-to-all-start.5 = ((bf16[64,64,256]{2,1,0:T(8,128)(2,1)}), bf16[64,64,256]{2,1,0:T(8,128)(2,1)S(1)}, u32[]{:S(2)}, u32[]{:S(2)}) async-start(bf16[64,64,256]{2,1,0:T(8,128)(2,1)} %copy-done.6), calls=%async_computation.5 | async-start | bytes 4194304 | tf_op jit(solution)/shard_map/all_to_all | solution.py:138
  53.0 1.3 copy-start.7
  96.7 1.3 copy-start.1
  98.0 57.1 %all-to-all-start.4 = ((bf16[64,64,256]{2,1,0:T(8,128)(2,1)}), bf16[64,64,256]{2,1,0:T(8,128)(2,1)}, u32[]{:S(2)}, u32[]{:S(2)}) async-start(bf16[64,64,256]{2,1,0:T(8,128)(2,1)} %copy-done.7), calls=%async_computation.4 | async-start | bytes 4194304 | tf_op jit(solution)/shard_map/all_to_all | solution.py:138
  110.6 1.3 copy-start.5
  155.2 57.0 %all-to-all-start.3 = ((bf16[64,64,256]{2,1,0:T(8,128)(2,1)}), bf16[64,64,256]{2,1,0:T(8,128)(2,1)S(1)}, u32[]{:S(2)}, u32[]{:S(2)}) async-start(bf16[64,64,256]{2,1,0:T(8,128)(2,1)} %copy-done.5), calls=%async_computation.3 | async-start | bytes 4194304 | tf_op jit(solution)/shard_map/all_to_all | solution.py:138
  167.5 1.3 copy-start.8
  168.9 50.6 %copy-start.9 = (bf16[1,2,256,256]{3,2,1,0:T(8,128)(2,1)S(1)}, bf16[1,2,256,256]{3,2,1,0:T(8,128)(2,1)}, u32[]{:S(2)}) copy-start(bf16[1,2,256,256]{3,2,1,0:T(8,128)(2,1)} %r_ref.1) | copy-start | bytes 786436
  168.9 50.6 %copy-start.12 = (s32[1,64]{1,0:T(1,128)S(1)}, s32[1,64]{1,0:T(1,128)}, u32[]{:S(2)}) copy-start(s32[1,64]{1,0:T(1,128)} %param.15) | copy-start | bytes 772
  168.9 50.6 %copy-start.13 = (s32[1,64]{1,0:T(1,128)S(1)}, s32[1,64]{1,0:T(1,128)}, u32[]{:S(2)}) copy-start(s32[1,64]{1,0:T(1,128)} %param.12) | copy-start | bytes 772
  212.2 1.4 copy-start.3
  213.6 57.0 %all-to-all-start.1 = ((bf16[64,64,256]{2,1,0:T(8,128)(2,1)}), bf16[64,64,256]{2,1,0:T(8,128)(2,1)S(1)}, u32[]{:S(2)}, u32[]{:S(2)}) async-start(bf16[64,64,256]{2,1,0:T(8,128)(2,1)} %copy-done.8), calls=%async_computation.1 | async-start | bytes 4194304 | tf_op jit(solution)/shard_map/all_to_all | solution.py:138
  219.5 1.6 copy-start.2
  227.1 9.4 %copy-start.4 = (bf16[64,64,256]{2,1,0:T(8,128)(2,1)S(1)}, bf16[64,64,256]{2,1,0:T(8,128)(2,1)}, u32[]{:S(2)}) copy-start(bf16[64,64,256]{2,1,0:T(8,128)(2,1)} %copy-done.3) | copy-start | bytes 6291460

commit v3 on v1

v3 whole, which is shorter than its diff:
```python
import functools

import jax
import jax.numpy as jnp
from jax import lax
from jax.experimental import pallas as pl
from jax.experimental.pallas import tpu as pltpu
from jax.sharding import PartitionSpec as P

CHUNK = 8
VMEM_LIMIT = 48 * 1024 * 1024


def _left_kernel(dep_ref, sector_ref, count_ref, m_ref, x_ref, o_ref):
    base = pl.program_id(0) * CHUNK
    for k in range(CHUNK):
        slot = dep_ref[base + k]
        prod = jnp.dot(
            m_ref[sector_ref[slot]], x_ref[slot], preferred_element_type=jnp.float32
        )
        o_ref[k] = jnp.where(slot < count_ref[0], prod, 0.0).astype(o_ref.dtype)


def apply_left(stacked, tiles, dep, left_sector, tile_count):
    n, w, _ = tiles.shape
    height = stacked.shape[1]
    spec = pltpu.PrefetchScalarGridSpec(
        num_scalar_prefetch=3,
        grid=(n // CHUNK,),
        in_specs=[
            pl.BlockSpec(stacked.shape, lambda c, *_: (0, 0, 0)),
            pl.BlockSpec(tiles.shape, lambda c, *_: (0, 0, 0)),
        ],
        out_specs=pl.BlockSpec((CHUNK, height, w), lambda c, *_: (c, 0, 0)),
    )
    return pl.pallas_call(
        _left_kernel,
        grid_spec=spec,
        out_shape=jax.ShapeDtypeStruct((n, height, w), jnp.bfloat16),
        compiler_params=pltpu.CompilerParams(vmem_limit_bytes=VMEM_LIMIT),
        cost_estimate=pl.CostEstimate(
            flops=2 * n * height * w * w,
            bytes_accessed=2 * (n * w * w + n * height * w + stacked.size),
            transcendentals=0,
        ),
    )(dep, left_sector, tile_count, stacked, tiles)


def _right_kernel(n_term, n_sector, arr_ref, rsel_ref, a_ref, rt_ref, o_ref):
    base = pl.program_id(0) * CHUNK
    rows = o_ref.shape[1]
    accs = [None] * n_sector
    for p in range(n_term):
        lhs = jnp.concatenate(
            [a_ref[arr_ref[base + k], pl.ds(p * rows, rows), :] for k in range(CHUNK)],
            axis=0,
        )
        for sector in range(n_sector):
            part = jnp.dot(
                lhs, rt_ref[p * n_sector + sector], preferred_element_type=jnp.float32
            )
            accs[sector] = part if accs[sector] is None else accs[sector] + part
    for k in range(CHUNK):
        chosen = rsel_ref[base + k]
        out = accs[n_sector - 1][k * rows:(k + 1) * rows]
        for sector in range(n_sector - 1):
            out = jnp.where(chosen == sector, accs[sector][k * rows:(k + 1) * rows], out)
        o_ref[k] = out.astype(o_ref.dtype)


def apply_right(placed, right_t, arr, rsel, n_term, n_sector):
    n, height, w = placed.shape
    rows = height // n_term
    spec = pltpu.PrefetchScalarGridSpec(
        num_scalar_prefetch=2,
        grid=(n // CHUNK,),
        in_specs=[
            pl.BlockSpec(placed.shape, lambda c, *_: (0, 0, 0)),
            pl.BlockSpec(right_t.shape, lambda c, *_: (0, 0, 0)),
        ],
        out_specs=pl.BlockSpec((CHUNK, rows, w), lambda c, *_: (c, 0, 0)),
    )
    return pl.pallas_call(
        functools.partial(_right_kernel, n_term, n_sector),
        grid_spec=spec,
        out_shape=jax.ShapeDtypeStruct((n, rows, w), jnp.bfloat16),
        compiler_params=pltpu.CompilerParams(vmem_limit_bytes=VMEM_LIMIT),
        cost_estimate=pl.CostEstimate(
            flops=2 * n_sector * n * height * w * w,
            bytes_accessed=2 * (n * height * w + right_t.size + n * rows * w),
            transcendentals=0,
        ),
    )(arr, rsel, placed, right_t)


def on_device(
    vectors, left_env, right_env, left_sector, right_sector, tile_count, departure, arrival
):
    n_term = lax.axis_size("term")
    me = lax.axis_index("term")
    n_vecs, tiles_dev, width, _ = vectors.shape
    n_sector = left_env.shape[1]
    rows = width // n_term

    own_left = left_env[0]
    own_right_t = jnp.swapaxes(right_env[0], 1, 2)
    left_parts = [lax.dynamic_slice_in_dim(own_left, me * rows, rows, axis=1)]
    right_parts = [own_right_t]
    for k in range(1, n_term):
        perm = [(i, (i + k) % n_term) for i in range(n_term)]
        dest = (me + k) % n_term
        send = lax.dynamic_slice_in_dim(own_left, dest * rows, rows, axis=1)
        left_parts.append(lax.ppermute(send, "term", perm))
        right_parts.append(lax.ppermute(own_right_t, "term", perm))
    stacked = jnp.concatenate(left_parts, axis=1)
    right_t = jnp.stack(right_parts).reshape(n_term * n_sector, width, width)

    outs = []
    for v in range(n_vecs):
        outgoing = apply_left(stacked, vectors[v], departure[0], left_sector[0], tile_count)
        incoming = lax.all_to_all(outgoing, "sec", split_axis=0, concat_axis=0, tiled=True)
        outs.append(apply_right(incoming, right_t, arrival[0], right_sector[0], n_term, n_sector))
    return jnp.stack(outs)


def solution(mesh):
    in_specs = (
        P(None, "sec", None, None),
        P("term", "sec", None, None),
        P("term", "sec", None, None),
        P("sec", None),
        P("sec", None),
        P("sec"),
        P("sec", None),
        P("sec", None),
    )
    out_specs = P(None, "sec", "term", None)
    return jax.shard_map(
        on_device, mesh=mesh, in_specs=in_specs, out_specs=out_specs, check_vma=False
    )
```

time: 247 us -> 231 us (0.935)
  blocking collectives: 210 us -> 0 us
  waiting for transfers between devices: 0.01 us -> 183 us
  starting transfers between devices: 3.52 us -> 23.4 us
  Pallas kernels: 26 us -> 20.7 us
    all_to_all x2 -> x0, blocking collectives: 210 us -> none  [the longest x1 200 us: on_device(): lax.all_to_all(outgoing, 'sec', split_axis=0, concat_axis=0, tiled=True)]
    all_to_all x1, waiting for transfers between devices: 0.01 us -> 170 us  [on_device(): lax.all_to_all(outgoing, 'sec', split_axis=0, concat_axis=0, tiled=True)]
    ppermute x0 -> x6, waiting for transfers between devices: none -> 13.2 us  [the longest x3 11.6 us: on_device(): right_parts.append(lax.ppermute(own_right_t, 'term', perm))]
    all_to_all x1, starting transfers between devices: 3.52 us -> 14.1 us  [on_device(): lax.all_to_all(outgoing, 'sec', split_axis=0, concat_axis=0, tiled=True)]
    ppermute x0 -> x6, starting transfers between devices: none -> 9.34 us  [the longest x3 5.71 us: on_device(): left_parts.append(lax.ppermute(send, 'term', perm))]
    pallas_call x1, Pallas kernels: 15.8 us -> 10.4 us  [apply_right(): pl.pallas_call(functools.partial(_right_kernel, n_term, n_sector), grid_s...]
  transfers between devices with their start and end apart: 1 -> 7, of which waited for: 0 -> 5; matrix products, arithmetic and copies ran while one was open for 1% -> 0% of each run, Pallas kernels for 4% -> 0%
where the time goes in v3:
time: 231 us
  waiting for transfers between devices  183 us (79%)
  starting transfers between devices  23.4 us (10%)
  Pallas kernels  20.7 us (9%)
  local copies, waits for them, and re-layouts  2.79 us (1%)
    all_to_all x1, waiting for transfers between devices, on_device(): lax.all_to_all(outgoing, 'sec', split_axis=0, concat_axis=0, tiled=True)  170 us
    all_to_all x1, starting transfers between devices, on_device(): lax.all_to_all(outgoing, 'sec', split_axis=0, concat_axis=0, tiled=True)  14.1 us
    ppermute x3, waiting for transfers between devices, on_device(): right_parts.append(lax.ppermute(own_right_t, 'term', perm))  11.6 us
    pallas_call x1, Pallas kernels, apply_right(): pl.pallas_call(functools.partial(_right_kernel, n_term, n_sector), grid_s...  10.4 us
    pallas_call x1, Pallas kernels, apply_left(): pl.pallas_call(_left_kernel, grid_spec=spec, out_shape=jax.ShapeDtypeStru...  10.3 us
    ppermute x3, starting transfers between devices, on_device(): left_parts.append(lax.ppermute(send, 'term', perm))  5.71 us
  transfers between devices with their start and end apart: 7, of which 5 were waited for; matrix products, arithmetic and copies ran while one was open for 0% of the time, Pallas kernels for 0%

profile of v3, /device:TPU:1, one launch (start us, length us, event | category | flops | bytes accessed | tf_op | source)
XLA Modules:
  0.0 230.8 jit_solution(2674453668686292522)
XLA Ops:
  0.0 1.0 dynamic-slice_bitcast_fusion.3
  1.0 2.1 collective-permute-start
  3.1 2.5 %collective-permute-start.1 = (bf16[2,64,256]{2,1,0:T(8,128)(2,1)S(1)}, bf16[2,64,256]{2,1,0:T(8,128)(2,1)S(1)}, u32[]{:S(2)}, u32[]{:S(2)}) collective-permute-start(bf16[2,64,256]{2,1,0:T(8,128)(2,1)S(1)} %get-tuple-element.8), channel_id=1, source_target_pairs={{0,128},{64,192},{128,0},{192,64},{1,129},{65,193},{129,1},{193,65... | collective-permute-start | bytes 196616 | tf_op jit(solution)/shard_map/ppermute | solution.py:113
  5.5 1.2 collective-permute-start.2
  7.3 0.0 collective-permute-done
  7.3 0.8 collective-permute-done.1
  8.1 0.8 collective-permute-done.2
  8.9 0.0 copy-start
  9.0 0.6 copy-done
  9.6 0.0 copy-start.1
  9.6 0.7 copy-done.1
  10.3 10.3 %shard_map.82 = bf16[64,256,256]{2,1,0:T(8,128)(2,1)} custom-call(s32[64]{0:T(128)S(1)} %bitcast.24, s32[64]{0:T(128)S(1)} %bitcast.25, s32[1]{0:T(128)S(6)} %copy.10.count_ref, bf16[2,256,256]{2,1,0:T(8,128)(2,1)S(1)} %pad_maximum_fusion.1.m_ref, bf16[64,256,256]{2,1,0:T(8,128)(2,1)} %bitcast.28), custom_call_target="tpu_custom_call" | custom-call | flops 2147483648 | bytes 17039360 | tf_op jit(solution)/shard_map/pallas_call | solution.py:36
  20.5 0.0 copy-start.4
  20.5 0.0 copy-start.2
  20.5 0.0 copy-start.3
  20.5 14.1 %all-to-all-start = ((bf16[64,256,256]{2,1,0:T(8,128)(2,1)}), bf16[64,256,256]{2,1,0:T(8,128)(2,1)}, u32[]{:S(2)}, u32[]{:S(2)}) async-start(bf16[64,256,256]{2,1,0:T(8,128)(2,1)} %shard_map.82), calls=%async_computation | async-start | bytes 16777216 | tf_op jit(solution)/shard_map/all_to_all | solution.py:121
  34.6 0.0 copy-done.4
  34.6 0.4 collective-permute-start.3
  35.0 3.3 %collective-permute-start.4 = (bf16[2,256,256]{1,2,0:T(8,128)(2,1)S(1)}, bf16[2,256,256]{1,2,0:T(8,128)(2,1)S(1)}, u32[]{:S(2)}, u32[]{:S(2)}) collective-permute-start(bf16[2,256,256]{1,2,0:T(8,128)(2,1)S(1)} %bitcast.30), channel_id=1, source_target_pairs={{0,128},{64,192},{128,0},{192,64},{1,129},{65,193},{129,1},{193,65... | collective-permute-start | bytes 786440 | tf_op jit(solution)/shard_map/ppermute | solution.py:114
  38.2 0.0 collective-permute-start.5
  38.3 5.1 %collective-permute-done.3 = bf16[2,256,256]{1,2,0:T(8,128)(2,1)S(1)} collective-permute-done((bf16[2,256,256]{1,2,0:T(8,128)(2,1)S(1)}, bf16[2,256,256]{1,2,0:T(8,128)(2,1)S(1)}, u32[]{:S(2)}, u32[]{:S(2)}) %collective-permute-start.3) | collective-permute-done | bytes 262176 | tf_op jit(solution)/shard_map/ppermute | solution.py:114
  43.3 6.5 %collective-permute-done.4 = bf16[2,256,256]{1,2,0:T(8,128)(2,1)S(1)} collective-permute-done((bf16[2,256,256]{1,2,0:T(8,128)(2,1)S(1)}, bf16[2,256,256]{1,2,0:T(8,128)(2,1)S(1)}, u32[]{:S(2)}, u32[]{:S(2)}) %collective-permute-start.4) | collective-permute-done | bytes 262176 | tf_op jit(solution)/shard_map/ppermute | solution.py:114
  49.8 0.0 collective-permute-done.5
  49.8 0.1 pad_maximum_fusion
  50.0 0.5 copy.9
  50.5 169.8 %all-to-all-done.a_ref = bf16[64,256,256]{2,1,0:T(8,128)(2,1)} async-done(((bf16[64,256,256]{2,1,0:T(8,128)(2,1)}), bf16[64,256,256]{2,1,0:T(8,128)(2,1)}, u32[]{:S(2)}, u32[]{:S(2)}) %all-to-all-start) | async-done | bytes 8388640 | tf_op jit(solution)/shard_map/all_to_all | solution.py:121
  220.3 0.0 copy-done.2
  220.3 0.0 copy-done.3
  220.4 10.4 %shard_map.83 = bf16[64,64,256]{2,1,0:T(8,128)(2,1)} custom-call(s32[64]{0:T(128)S(1)} %bitcast.26, s32[64]{0:T(128)S(1)} %bitcast.27, bf16[64,256,256]{2,1,0:T(8,128)(2,1)} %all-to-all-done.a_ref, bf16[8,256,256]{2,1,0:T(8,128)(2,1)S(1)} %bitcast.23), custom_call_target="tpu_custom_call" | custom-call | flops 4294967296 | bytes 11534336 | tf_op jit(solution)/shard_map/pallas_call | solution.py:83
  (1 shorter events, 0.0 us)
Async XLA Ops:
  1.0 6.4 %collective-permute-start = (bf16[2,64,256]{2,1,0:T(8,128)(2,1)S(1)}, bf16[2,64,256]{2,1,0:T(8,128)(2,1)S(1)}, u32[]{:S(2)}, u32[]{:S(2)}) collective-permute-start(bf16[2,64,256]{2,1,0:T(8,128)(2,1)S(1)} %get-tuple-element.6), channel_id=1, source_target_pairs={{0,64},{64,128},{128,192},{192,0},{1,65},{65,129},{129,193},{193,1... | collective-permute-start | bytes 196616 | tf_op jit(solution)/shard_map/ppermute | solution.py:113
  3.1 5.1 %collective-permute-start.1 = (bf16[2,64,256]{2,1,0:T(8,128)(2,1)S(1)}, bf16[2,64,256]{2,1,0:T(8,128)(2,1)S(1)}, u32[]{:S(2)}, u32[]{:S(2)}) collective-permute-start(bf16[2,64,256]{2,1,0:T(8,128)(2,1)S(1)} %get-tuple-element.8), channel_id=1, source_target_pairs={{0,128},{64,192},{128,0},{192,64},{1,129},{65,193},{129,1},{193,65... | collective-permute-start | bytes 196616 | tf_op jit(solution)/shard_map/ppermute | solution.py:113
  5.5 3.4 %collective-permute-start.2 = (bf16[2,64,256]{2,1,0:T(8,128)(2,1)S(1)}, bf16[2,64,256]{2,1,0:T(8,128)(2,1)S(1)}, u32[]{:S(2)}, u32[]{:S(2)}) collective-permute-start(bf16[2,64,256]{2,1,0:T(8,128)(2,1)S(1)} %get-tuple-element.7), channel_id=1, source_target_pairs={{0,192},{64,0},{128,64},{192,128},{1,193},{65,1},{129,65},{193,129... | collective-permute-start | bytes 196616 | tf_op jit(solution)/shard_map/ppermute | solution.py:113
  8.9 0.7 copy-start
  9.6 0.7 copy-start.1
  20.5 14.1 %copy-start.4 = (bf16[1,2,256,256]{3,2,1,0:T(8,128)(2,1)S(1)}, bf16[1,2,256,256]{3,2,1,0:T(8,128)(2,1)}, u32[]{:S(2)}) copy-start(bf16[1,2,256,256]{3,2,1,0:T(8,128)(2,1)} %param.10) | copy-start | bytes 786436
  20.5 199.8 %copy-start.2 = (s32[1,64]{1,0:T(1,128)S(1)}, s32[1,64]{1,0:T(1,128)}, u32[]{:S(2)}) copy-start(s32[1,64]{1,0:T(1,128)} %param.15) | copy-start | bytes 772
  20.5 199.8 %copy-start.3 = (s32[1,64]{1,0:T(1,128)S(1)}, s32[1,64]{1,0:T(1,128)}, u32[]{:S(2)}) copy-start(s32[1,64]{1,0:T(1,128)} %param.12) | copy-start | bytes 772
  20.5 199.8 %all-to-all-start = ((bf16[64,256,256]{2,1,0:T(8,128)(2,1)}), bf16[64,256,256]{2,1,0:T(8,128)(2,1)}, u32[]{:S(2)}, u32[]{:S(2)}) async-start(bf16[64,256,256]{2,1,0:T(8,128)(2,1)} %shard_map.82), calls=%async_computation | async-start | bytes 16777216 | tf_op jit(solution)/shard_map/all_to_all | solution.py:121
  34.6 8.7 %collective-permute-start.3 = (bf16[2,256,256]{1,2,0:T(8,128)(2,1)S(1)}, bf16[2,256,256]{1,2,0:T(8,128)(2,1)S(1)}, u32[]{:S(2)}, u32[]{:S(2)}) collective-permute-start(bf16[2,256,256]{1,2,0:T(8,128)(2,1)S(1)} %bitcast.29), channel_id=1, source_target_pairs={{0,64},{64,128},{128,192},{192,0},{1,65},{65,129},{129,193},{193,1... | collective-permute-start | bytes 786440 | tf_op jit(solution)/shard_map/ppermute | solution.py:114
  35.0 14.8 %collective-permute-start.4 = (bf16[2,256,256]{1,2,0:T(8,128)(2,1)S(1)}, bf16[2,256,256]{1,2,0:T(8,128)(2,1)S(1)}, u32[]{:S(2)}, u32[]{:S(2)}) collective-permute-start(bf16[2,256,256]{1,2,0:T(8,128)(2,1)S(1)} %bitcast.30), channel_id=1, source_target_pairs={{0,128},{64,192},{128,0},{192,64},{1,129},{65,193},{129,1},{193,65... | collective-permute-start | bytes 786440 | tf_op jit(solution)/shard_map/ppermute | solution.py:114
  38.2 11.6 %collective-permute-start.5 = (bf16[2,256,256]{1,2,0:T(8,128)(2,1)S(1)}, bf16[2,256,256]{1,2,0:T(8,128)(2,1)S(1)}, u32[]{:S(2)}, u32[]{:S(2)}) collective-permute-start(bf16[2,256,256]{1,2,0:T(8,128)(2,1)S(1)} %bitcast.31), channel_id=1, source_target_pairs={{0,192},{64,0},{128,64},{192,128},{1,193},{65,1},{129,65},{193,129... | collective-permute-start | bytes 786440 | tf_op jit(solution)/shard_map/ppermute | solution.py:114

commit v4 on v3

v4 whole, which is shorter than its diff:
```python
import functools

import jax
import jax.numpy as jnp
from jax import lax
from jax.experimental import pallas as pl
from jax.experimental.pallas import tpu as pltpu
from jax.sharding import PartitionSpec as P

CHUNK = 8
VMEM_LIMIT = 48 * 1024 * 1024


def _left_kernel(dep_ref, sector_ref, count_ref, m_ref, x_ref, o_ref):
    base = pl.program_id(0) * CHUNK
    n_term, _, rows, _ = o_ref.shape
    for k in range(CHUNK):
        slot = dep_ref[base + k]
        prod = jnp.dot(
            m_ref[sector_ref[slot]], x_ref[slot], preferred_element_type=jnp.float32
        )
        prod = jnp.where(slot < count_ref[0], prod, 0.0).astype(o_ref.dtype)
        for p in range(n_term):
            o_ref[p, k] = prod[p * rows:(p + 1) * rows]


def apply_left(blocks, tiles, dep, left_sector, tile_count, n_term):
    n, w, _ = tiles.shape
    rows = w // n_term
    spec = pltpu.PrefetchScalarGridSpec(
        num_scalar_prefetch=3,
        grid=(n // CHUNK,),
        in_specs=[
            pl.BlockSpec(blocks.shape, lambda c, *_: (0, 0, 0)),
            pl.BlockSpec(tiles.shape, lambda c, *_: (0, 0, 0)),
        ],
        out_specs=pl.BlockSpec((n_term, CHUNK, rows, w), lambda c, *_: (0, c, 0, 0)),
    )
    return pl.pallas_call(
        _left_kernel,
        grid_spec=spec,
        out_shape=jax.ShapeDtypeStruct((n_term, n, rows, w), jnp.bfloat16),
        compiler_params=pltpu.CompilerParams(vmem_limit_bytes=VMEM_LIMIT),
        cost_estimate=pl.CostEstimate(
            flops=2 * n * w * w * w,
            bytes_accessed=2 * (2 * n * w * w + blocks.size),
            transcendentals=0,
        ),
    )(dep, left_sector, tile_count, blocks, tiles)


def _right_kernel(n_term, n_sector, arr_ref, rsel_ref, me_ref, a_ref, rt_ref, o_ref):
    base = pl.program_id(0) * CHUNK
    rows = o_ref.shape[1]
    per_term = a_ref.shape[0] // n_term
    accs = [None] * n_sector
    for k in range(n_term):
        origin = lax.rem(me_ref[0] + (n_term - k), n_term) * per_term
        lhs = jnp.concatenate(
            [a_ref[origin + arr_ref[base + q]] for q in range(CHUNK)], axis=0
        )
        for sector in range(n_sector):
            part = jnp.dot(
                lhs, rt_ref[k * n_sector + sector], preferred_element_type=jnp.float32
            )
            accs[sector] = part if accs[sector] is None else accs[sector] + part
    for q in range(CHUNK):
        chosen = rsel_ref[base + q]
        out = accs[n_sector - 1][q * rows:(q + 1) * rows]
        for sector in range(n_sector - 1):
            out = jnp.where(chosen == sector, accs[sector][q * rows:(q + 1) * rows], out)
        o_ref[q] = out.astype(o_ref.dtype)


def apply_right(incoming, right_t, arr, rsel, me, n_term, n_sector):
    total, rows, w = incoming.shape
    n = arr.shape[0]
    spec = pltpu.PrefetchScalarGridSpec(
        num_scalar_prefetch=3,
        grid=(n // CHUNK,),
        in_specs=[
            pl.BlockSpec(incoming.shape, lambda c, *_: (0, 0, 0)),
            pl.BlockSpec(right_t.shape, lambda c, *_: (0, 0, 0)),
        ],
        out_specs=pl.BlockSpec((CHUNK, rows, w), lambda c, *_: (c, 0, 0)),
    )
    return pl.pallas_call(
        functools.partial(_right_kernel, n_term, n_sector),
        grid_spec=spec,
        out_shape=jax.ShapeDtypeStruct((n, rows, w), jnp.bfloat16),
        compiler_params=pltpu.CompilerParams(vmem_limit_bytes=VMEM_LIMIT),
        cost_estimate=pl.CostEstimate(
            flops=2 * n_sector * total * rows * w * w,
            bytes_accessed=2 * (total * rows * w + right_t.size + n * rows * w),
            transcendentals=0,
        ),
    )(arr, rsel, me, incoming, right_t)


def on_device(
    vectors, left_env, right_env, left_sector, right_sector, tile_count, departure, arrival
):
    n_term = lax.axis_size("term")
    me = lax.axis_index("term")
    n_vecs, tiles_dev, width, _ = vectors.shape
    n_sector = left_env.shape[1]
    rows = width // n_term

    own_right_t = jnp.swapaxes(right_env[0], 1, 2)
    right_parts = [own_right_t]
    for k in range(1, n_term):
        perm = [(i, (i + k) % n_term) for i in range(n_term)]
        right_parts.append(lax.ppermute(own_right_t, "term", perm))
    right_t = jnp.stack(right_parts).reshape(n_term * n_sector, width, width)
    me_arr = jnp.reshape(me, (1,)).astype(jnp.int32)

    outs = []
    for v in range(n_vecs):
        outgoing = apply_left(
            left_env[0], vectors[v], departure[0], left_sector[0], tile_count, n_term
        )
        incoming = lax.all_to_all(
            outgoing.reshape(n_term * tiles_dev, rows, width),
            ("term", "sec"), split_axis=0, concat_axis=0, tiled=True,
        )
        outs.append(
            apply_right(incoming, right_t, arrival[0], right_sector[0], me_arr, n_term, n_sector)
        )
    return jnp.stack(outs)


def solution(mesh):
    in_specs = (
        P(None, "sec", None, None),
        P("term", "sec", None, None),
        P("term", "sec", None, None),
        P("sec", None),
        P("sec", None),
        P("sec"),
        P("sec", None),
        P("sec", None),
    )
    out_specs = P(None, "sec", "term", None)
    return jax.shard_map(
        on_device, mesh=mesh, in_specs=in_specs, out_specs=out_specs, check_vma=False
    )
```

time: 231 us -> 229 us (level)
  starting transfers between devices: 23.4 us -> 20.4 us
    ppermute x3, waiting for transfers between devices: 11.6 us -> 33.7 us  [on_device(): right_parts.append(lax.ppermute(own_right_t, 'term', perm))]
    all_to_all x1, waiting for transfers between devices: 170 us -> 150 us  [on_device(): lax.all_to_all(outgoing.reshape(n_term * tiles_dev, rows, width), ('term'...]
    ppermute x3 -> x0, starting transfers between devices: 5.71 us -> none  [on_device(): left_parts.append(lax.ppermute(send, 'term', perm))]
    all_to_all x1, starting transfers between devices: 14.1 us -> 16.7 us  [on_device(): lax.all_to_all(outgoing.reshape(n_term * tiles_dev, rows, width), ('term'...]
  transfers between devices with their start and end apart: 7 -> 4, of which waited for: 5 -> 4; matrix products, arithmetic and copies ran while one was open for 0% -> 0% of each run, Pallas kernels for 0% -> 0%
where the time goes in v4:
time: 229 us
  waiting for transfers between devices  184 us (80%)
  Pallas kernels  20.6 us (9%)
  starting transfers between devices  20.4 us (9%)
  local copies, waits for them, and re-layouts  2.79 us (1%)
    all_to_all x1, waiting for transfers between devices, on_device(): lax.all_to_all(outgoing.reshape(n_term * tiles_dev, rows, width), ('term'...  150 us
    ppermute x3, waiting for transfers between devices, on_device(): right_parts.append(lax.ppermute(own_right_t, 'term', perm))  33.7 us
    all_to_all x1, starting transfers between devices, on_device(): lax.all_to_all(outgoing.reshape(n_term * tiles_dev, rows, width), ('term'...  16.7 us
    pallas_call x1, Pallas kernels, apply_right(): pl.pallas_call(functools.partial(_right_kernel, n_term, n_sector), grid_s...  10.4 us
    pallas_call x1, Pallas kernels, apply_left(): pl.pallas_call(_left_kernel, grid_spec=spec, out_shape=jax.ShapeDtypeStru...  10.2 us
  transfers between devices with their start and end apart: 4, of which 4 were waited for; matrix products, arithmetic and copies ran while one was open for 0% of the time, Pallas kernels for 0%

profile of v4, /device:TPU:1, one launch (start us, length us, event | category | flops | bytes accessed | tf_op | source)
XLA Modules:
  0.0 228.6 jit_solution(15951826299865262978)
XLA Ops:
  0.7 0.0 copy-start
  0.7 0.9 copy-done
  1.6 0.0 copy-start.1
  1.6 0.7 copy-done.1
  2.3 0.0 copy-start.2
  2.3 0.7 copy-done.2
  2.9 10.2 %shard_map.82 = bf16[4,64,64,256]{3,2,1,0:T(8,128)(2,1)} custom-call(s32[64]{0:T(128)S(1)} %bitcast.20, s32[64]{0:T(128)S(1)} %bitcast.21, s32[1]{0:T(128)S(6)} %copy.10.count_ref, bf16[2,256,256]{2,1,0:T(8,128)(2,1)S(1)} %bitcast.19, bf16[64,256,256]{2,1,0:T(8,128)(2,1)} %bitcast.25), custom_call_target="tpu_custom_call" | custom-call | flops 2147483648 | bytes 17039360 | tf_op jit(solution)/shard_map/pallas_call | solution.py:39
  13.1 0.0 copy-start.5
  13.1 0.0 copy-start.3
  13.1 0.0 copy-start.4
  13.1 16.7 %all-to-all-start = ((bf16[256,64,256]{2,1,0:T(8,128)(2,1)}), bf16[256,64,256]{2,1,0:T(8,128)(2,1)}, u32[]{:S(2)}, u32[]{:S(2)}) async-start(bf16[256,64,256]{2,1,0:T(8,128)(2,1)} %bitcast.24), calls=%async_computation | async-start | bytes 16777216 | tf_op jit(solution)/shard_map/all_to_all | solution.py:122
  29.8 0.0 copy-done.5
  29.8 2.6 %collective-permute-start.2 = (bf16[2,256,256]{1,2,0:T(8,128)(2,1)S(1)}, bf16[2,256,256]{1,2,0:T(8,128)(2,1)S(1)}, u32[]{:S(2)}, u32[]{:S(2)}) collective-permute-start(bf16[2,256,256]{1,2,0:T(8,128)(2,1)S(1)} %bitcast.26), channel_id=1, source_target_pairs={{0,192},{64,0},{128,64},{192,128},{1,193},{65,1},{129,65},{193,129... | collective-permute-start | bytes 786440 | tf_op jit(solution)/shard_map/ppermute | solution.py:113
  32.4 0.6 collective-permute-start.1
  33.0 0.6 collective-permute-start
  33.6 23.2 %collective-permute-done.2 = bf16[2,256,256]{1,2,0:T(8,128)(2,1)S(1)} collective-permute-done((bf16[2,256,256]{1,2,0:T(8,128)(2,1)S(1)}, bf16[2,256,256]{1,2,0:T(8,128)(2,1)S(1)}, u32[]{:S(2)}, u32[]{:S(2)}) %collective-permute-start.2) | collective-permute-done | bytes 262176 | tf_op jit(solution)/shard_map/ppermute | solution.py:113
  56.7 0.4 collective-permute-done.1
  57.2 10.1 %collective-permute-done = bf16[2,256,256]{1,2,0:T(8,128)(2,1)S(1)} collective-permute-done((bf16[2,256,256]{1,2,0:T(8,128)(2,1)S(1)}, bf16[2,256,256]{1,2,0:T(8,128)(2,1)S(1)}, u32[]{:S(2)}, u32[]{:S(2)}) %collective-permute-start) | collective-permute-done | bytes 262176 | tf_op jit(solution)/shard_map/ppermute | solution.py:113
  67.3 0.1 pad_maximum_fusion
  67.4 0.5 copy.9
  68.0 150.2 %all-to-all-done.a_ref = bf16[256,64,256]{2,1,0:T(8,128)(2,1)} async-done(((bf16[256,64,256]{2,1,0:T(8,128)(2,1)}), bf16[256,64,256]{2,1,0:T(8,128)(2,1)}, u32[]{:S(2)}, u32[]{:S(2)}) %all-to-all-start) | async-done | bytes 8388640 | tf_op jit(solution)/shard_map/all_to_all | solution.py:122
  218.2 0.0 copy-done.3
  218.2 0.0 copy-done.4
  218.2 10.4 %shard_map.83 = bf16[64,64,256]{2,1,0:T(8,128)(2,1)} custom-call(s32[64]{0:T(128)S(1)} %bitcast.22, s32[64]{0:T(128)S(1)} %bitcast.23, s32[1]{0:T(128)} %bitcast.2.me_ref, bf16[256,64,256]{2,1,0:T(8,128)(2,1)} %all-to-all-done.a_ref, bf16[8,256,256]{2,1,0:T(8,128)(2,1)S(1)} %bitcast.18), custom_call_target="tpu_custom_call" | custom-call | flops 4294967296 | bytes 11534336 | tf_op jit(solution)/shard_map/pallas_call | solution.py:87
Async XLA Ops:
  0.7 1.0 copy-start
  1.6 0.7 copy-start.1
  2.3 0.7 copy-start.2
  13.1 16.7 %copy-start.5 = (bf16[1,2,256,256]{3,2,1,0:T(8,128)(2,1)S(1)}, bf16[1,2,256,256]{3,2,1,0:T(8,128)(2,1)}, u32[]{:S(2)}) copy-start(bf16[1,2,256,256]{3,2,1,0:T(8,128)(2,1)} %param.10) | copy-start | bytes 786436
  13.1 205.1 %copy-start.3 = (s32[1,64]{1,0:T(1,128)S(1)}, s32[1,64]{1,0:T(1,128)}, u32[]{:S(2)}) copy-start(s32[1,64]{1,0:T(1,128)} %param.15) | copy-start | bytes 772
  13.1 205.1 %copy-start.4 = (s32[1,64]{1,0:T(1,128)S(1)}, s32[1,64]{1,0:T(1,128)}, u32[]{:S(2)}) copy-start(s32[1,64]{1,0:T(1,128)} %param.12) | copy-start | bytes 772
  13.1 205.1 %all-to-all-start = ((bf16[256,64,256]{2,1,0:T(8,128)(2,1)}), bf16[256,64,256]{2,1,0:T(8,128)(2,1)}, u32[]{:S(2)}, u32[]{:S(2)}) async-start(bf16[256,64,256]{2,1,0:T(8,128)(2,1)} %bitcast.24), calls=%async_computation | async-start | bytes 16777216 | tf_op jit(solution)/shard_map/all_to_all | solution.py:122
  29.8 27.0 %collective-permute-start.2 = (bf16[2,256,256]{1,2,0:T(8,128)(2,1)S(1)}, bf16[2,256,256]{1,2,0:T(8,128)(2,1)S(1)}, u32[]{:S(2)}, u32[]{:S(2)}) collective-permute-start(bf16[2,256,256]{1,2,0:T(8,128)(2,1)S(1)} %bitcast.26), channel_id=1, source_target_pairs={{0,192},{64,0},{128,64},{192,128},{1,193},{65,1},{129,65},{193,129... | collective-permute-start | bytes 786440 | tf_op jit(solution)/shard_map/ppermute | solution.py:113
  32.4 24.8 %collective-permute-start.1 = (bf16[2,256,256]{1,2,0:T(8,128)(2,1)S(1)}, bf16[2,256,256]{1,2,0:T(8,128)(2,1)S(1)}, u32[]{:S(2)}, u32[]{:S(2)}) collective-permute-start(bf16[2,256,256]{1,2,0:T(8,128)(2,1)S(1)} %bitcast.27), channel_id=1, source_target_pairs={{0,128},{64,192},{128,0},{192,64},{1,129},{65,193},{129,1},{193,65... | collective-permute-start | bytes 786440 | tf_op jit(solution)/shard_map/ppermute | solution.py:113
  33.0 34.3 %collective-permute-start = (bf16[2,256,256]{1,2,0:T(8,128)(2,1)S(1)}, bf16[2,256,256]{1,2,0:T(8,128)(2,1)S(1)}, u32[]{:S(2)}, u32[]{:S(2)}) collective-permute-start(bf16[2,256,256]{1,2,0:T(8,128)(2,1)S(1)} %bitcast.28), channel_id=1, source_target_pairs={{0,64},{64,128},{128,192},{192,0},{1,65},{65,129},{129,193},{193,1... | collective-permute-start | bytes 786440 | tf_op jit(solution)/shard_map/ppermute | solution.py:113

commit v5 on v4

--- a/solution.py
+++ b/solution.py
@@ -7,14 +7,15 @@
 from jax.experimental.pallas import tpu as pltpu
 from jax.sharding import PartitionSpec as P
 
-CHUNK = 8
+LEFT_CHUNK = 16
+RIGHT_CHUNK = 32
 VMEM_LIMIT = 48 * 1024 * 1024
 
 
 def _left_kernel(dep_ref, sector_ref, count_ref, m_ref, x_ref, o_ref):
-    base = pl.program_id(0) * CHUNK
+    base = pl.program_id(0) * LEFT_CHUNK
     n_term, _, rows, _ = o_ref.shape
-    for k in range(CHUNK):
+    for k in range(LEFT_CHUNK):
         slot = dep_ref[base + k]
         prod = jnp.dot(
             m_ref[sector_ref[slot]], x_ref[slot], preferred_element_type=jnp.float32
@@ -29,12 +30,12 @@
     rows = w // n_term
     spec = pltpu.PrefetchScalarGridSpec(
         num_scalar_prefetch=3,
-        grid=(n // CHUNK,),
+        grid=(n // LEFT_CHUNK,),
         in_specs=[
             pl.BlockSpec(blocks.shape, lambda c, *_: (0, 0, 0)),
             pl.BlockSpec(tiles.shape, lambda c, *_: (0, 0, 0)),
         ],
-        out_specs=pl.BlockSpec((n_term, CHUNK, rows, w), lambda c, *_: (0, c, 0, 0)),
+        out_specs=pl.BlockSpec((n_term, LEFT_CHUNK, rows, w), lambda c, *_: (0, c, 0, 0)),
     )
     return pl.pallas_call(
         _left_kernel,
@@ -50,21 +51,21 @@
 
 
 def _right_kernel(n_term, n_sector, arr_ref, rsel_ref, me_ref, a_ref, rt_ref, o_ref):
-    base = pl.program_id(0) * CHUNK
+    base = pl.program_id(0) * RIGHT_CHUNK
     rows = o_ref.shape[1]
     per_term = a_ref.shape[0] // n_term
     accs = [None] * n_sector
     for k in range(n_term):
         origin = lax.rem(me_ref[0] + (n_term - k), n_term) * per_term
         lhs = jnp.concatenate(
-            [a_ref[origin + arr_ref[base + q]] for q in range(CHUNK)], axis=0
+            [a_ref[origin + arr_ref[base + q]] for q in range(RIGHT_CHUNK)], axis=0
         )
         for sector in range(n_sector):
             part = jnp.dot(
                 lhs, rt_ref[k * n_sector + sector], preferred_element_type=jnp.float32
             )
             accs[sector] = part if accs[sector] is None else accs[sector] + part
-    for q in range(CHUNK):
+    for q in range(RIGHT_CHUNK):
         chosen = rsel_ref[base + q]
         out = accs[n_sector - 1][q * rows:(q + 1) * rows]
         for sector in range(n_sector - 1):
@@ -77,12 +78,12 @@
     n = arr.shape[0]
     spec = pltpu.PrefetchScalarGridSpec(
         num_scalar_prefetch=3,
-        grid=(n // CHUNK,),
+        grid=(n // RIGHT_CHUNK,),
         in_specs=[
             pl.BlockSpec(incoming.shape, lambda c, *_: (0, 0, 0)),
             pl.BlockSpec(right_t.shape, lambda c, *_: (0, 0, 0)),
         ],
-        out_specs=pl.BlockSpec((CHUNK, rows, w), lambda c, *_: (c, 0, 0)),
+        out_specs=pl.BlockSpec((RIGHT_CHUNK, rows, w), lambda c, *_: (c, 0, 0)),
     )
     return pl.pallas_call(
         functools.partial(_right_kernel, n_term, n_sector),

time: 229 us -> 227 us (level)
  no operation moved by 1% of the time
where the time goes in v5:
time: 227 us
  waiting for transfers between devices  184 us (81%)
  starting transfers between devices  20.4 us (9%)
  Pallas kernels  18.6 us (8%)
  local copies, waits for them, and re-layouts  2.79 us (1%)
    all_to_all x1, waiting for transfers between devices, on_device(): lax.all_to_all(outgoing.reshape(n_term * tiles_dev, rows, width), ('term'...  150 us
    ppermute x3, waiting for transfers between devices, on_device(): right_parts.append(lax.ppermute(own_right_t, 'term', perm))  33.7 us
    all_to_all x1, starting transfers between devices, on_device(): lax.all_to_all(outgoing.reshape(n_term * tiles_dev, rows, width), ('term'...  16.6 us
    pallas_call x1, Pallas kernels, apply_right(): pl.pallas_call(functools.partial(_right_kernel, n_term, n_sector), grid_s...  9.86 us
    pallas_call x1, Pallas kernels, apply_left(): pl.pallas_call(_left_kernel, grid_spec=spec, out_shape=jax.ShapeDtypeStru...  8.78 us
  transfers between devices with their start and end apart: 4, of which 4 were waited for; matrix products, arithmetic and copies ran while one was open for 0% of the time, Pallas kernels for 0%

profile of v5, /device:TPU:1, one launch (start us, length us, event | category | flops | bytes accessed | tf_op | source)
XLA Modules:
  0.0 226.6 jit_solution(4381979716014253767)
XLA Ops:
  0.7 0.0 copy-start
  0.7 0.9 copy-done
  1.6 0.0 copy-start.1
  1.6 0.7 copy-done.1
  2.3 0.0 copy-start.2
  2.3 0.7 copy-done.2
  2.9 8.8 %shard_map.82 = bf16[4,64,64,256]{3,2,1,0:T(8,128)(2,1)} custom-call(s32[64]{0:T(128)S(1)} %bitcast.20, s32[64]{0:T(128)S(1)} %bitcast.21, s32[1]{0:T(128)S(6)} %copy.10.count_ref, bf16[2,256,256]{2,1,0:T(8,128)(2,1)S(1)} %bitcast.19, bf16[64,256,256]{2,1,0:T(8,128)(2,1)} %bitcast.25), custom_call_target="tpu_custom_call" | custom-call | flops 2147483648 | bytes 17039360 | tf_op jit(solution)/shard_map/pallas_call | solution.py:40
  11.7 0.0 copy-start.5
  11.7 0.0 copy-start.3
  11.7 0.0 copy-start.4
  11.7 16.6 %all-to-all-start = ((bf16[256,64,256]{2,1,0:T(8,128)(2,1)}), bf16[256,64,256]{2,1,0:T(8,128)(2,1)}, u32[]{:S(2)}, u32[]{:S(2)}) async-start(bf16[256,64,256]{2,1,0:T(8,128)(2,1)} %bitcast.24), calls=%async_computation | async-start | bytes 16777216 | tf_op jit(solution)/shard_map/all_to_all | solution.py:123
  28.4 0.0 copy-done.5
  28.4 2.6 %collective-permute-start.2 = (bf16[2,256,256]{1,2,0:T(8,128)(2,1)S(1)}, bf16[2,256,256]{1,2,0:T(8,128)(2,1)S(1)}, u32[]{:S(2)}, u32[]{:S(2)}) collective-permute-start(bf16[2,256,256]{1,2,0:T(8,128)(2,1)S(1)} %bitcast.26), channel_id=1, source_target_pairs={{0,192},{64,0},{128,64},{192,128},{1,193},{65,1},{129,65},{193,129... | collective-permute-start | bytes 786440 | tf_op jit(solution)/shard_map/ppermute | solution.py:114
  31.0 0.6 collective-permute-start.1
  31.6 0.6 collective-permute-start
  32.2 23.2 %collective-permute-done.2 = bf16[2,256,256]{1,2,0:T(8,128)(2,1)S(1)} collective-permute-done((bf16[2,256,256]{1,2,0:T(8,128)(2,1)S(1)}, bf16[2,256,256]{1,2,0:T(8,128)(2,1)S(1)}, u32[]{:S(2)}, u32[]{:S(2)}) %collective-permute-start.2) | collective-permute-done | bytes 262176 | tf_op jit(solution)/shard_map/ppermute | solution.py:114
  55.3 0.4 collective-permute-done.1
  55.8 10.1 %collective-permute-done = bf16[2,256,256]{1,2,0:T(8,128)(2,1)S(1)} collective-permute-done((bf16[2,256,256]{1,2,0:T(8,128)(2,1)S(1)}, bf16[2,256,256]{1,2,0:T(8,128)(2,1)S(1)}, u32[]{:S(2)}, u32[]{:S(2)}) %collective-permute-start) | collective-permute-done | bytes 262176 | tf_op jit(solution)/shard_map/ppermute | solution.py:114
  65.9 0.1 pad_maximum_fusion
  66.0 0.5 copy.9
  66.6 150.2 %all-to-all-done.a_ref = bf16[256,64,256]{2,1,0:T(8,128)(2,1)} async-done(((bf16[256,64,256]{2,1,0:T(8,128)(2,1)}), bf16[256,64,256]{2,1,0:T(8,128)(2,1)}, u32[]{:S(2)}, u32[]{:S(2)}) %all-to-all-start) | async-done | bytes 8388640 | tf_op jit(solution)/shard_map/all_to_all | solution.py:123
  216.8 0.0 copy-done.3
  216.8 0.0 copy-done.4
  216.8 9.9 %shard_map.83 = bf16[64,64,256]{2,1,0:T(8,128)(2,1)} custom-call(s32[64]{0:T(128)S(1)} %bitcast.22, s32[64]{0:T(128)S(1)} %bitcast.23, s32[1]{0:T(128)} %bitcast.2.me_ref, bf16[256,64,256]{2,1,0:T(8,128)(2,1)} %all-to-all-done.a_ref, bf16[8,256,256]{2,1,0:T(8,128)(2,1)S(1)} %bitcast.18), custom_call_target="tpu_custom_call" | custom-call | flops 4294967296 | bytes 11534336 | tf_op jit(solution)/shard_map/pallas_call | solution.py:88
Async XLA Ops:
  0.7 1.0 copy-start
  1.6 0.7 copy-start.1
  2.3 0.7 copy-start.2
  11.7 16.7 %copy-start.5 = (bf16[1,2,256,256]{3,2,1,0:T(8,128)(2,1)S(1)}, bf16[1,2,256,256]{3,2,1,0:T(8,128)(2,1)}, u32[]{:S(2)}) copy-start(bf16[1,2,256,256]{3,2,1,0:T(8,128)(2,1)} %param.10) | copy-start | bytes 786436
  11.7 205.1 %copy-start.3 = (s32[1,64]{1,0:T(1,128)S(1)}, s32[1,64]{1,0:T(1,128)}, u32[]{:S(2)}) copy-start(s32[1,64]{1,0:T(1,128)} %param.15) | copy-start | bytes 772
  11.7 205.1 %copy-start.4 = (s32[1,64]{1,0:T(1,128)S(1)}, s32[1,64]{1,0:T(1,128)}, u32[]{:S(2)}) copy-start(s32[1,64]{1,0:T(1,128)} %param.12) | copy-start | bytes 772
  11.7 205.1 %all-to-all-start = ((bf16[256,64,256]{2,1,0:T(8,128)(2,1)}), bf16[256,64,256]{2,1,0:T(8,128)(2,1)}, u32[]{:S(2)}, u32[]{:S(2)}) async-start(bf16[256,64,256]{2,1,0:T(8,128)(2,1)} %bitcast.24), calls=%async_computation | async-start | bytes 16777216 | tf_op jit(solution)/shard_map/all_to_all | solution.py:123
  28.4 27.0 %collective-permute-start.2 = (bf16[2,256,256]{1,2,0:T(8,128)(2,1)S(1)}, bf16[2,256,256]{1,2,0:T(8,128)(2,1)S(1)}, u32[]{:S(2)}, u32[]{:S(2)}) collective-permute-start(bf16[2,256,256]{1,2,0:T(8,128)(2,1)S(1)} %bitcast.26), channel_id=1, source_target_pairs={{0,192},{64,0},{128,64},{192,128},{1,193},{65,1},{129,65},{193,129... | collective-permute-start | bytes 786440 | tf_op jit(solution)/shard_map/ppermute | solution.py:114
  31.0 24.8 %collective-permute-start.1 = (bf16[2,256,256]{1,2,0:T(8,128)(2,1)S(1)}, bf16[2,256,256]{1,2,0:T(8,128)(2,1)S(1)}, u32[]{:S(2)}, u32[]{:S(2)}) collective-permute-start(bf16[2,256,256]{1,2,0:T(8,128)(2,1)S(1)} %bitcast.27), channel_id=1, source_target_pairs={{0,128},{64,192},{128,0},{192,64},{1,129},{65,193},{129,1},{193,65... | collective-permute-start | bytes 786440 | tf_op jit(solution)/shard_map/ppermute | solution.py:114
  31.6 34.3 %collective-permute-start = (bf16[2,256,256]{1,2,0:T(8,128)(2,1)S(1)}, bf16[2,256,256]{1,2,0:T(8,128)(2,1)S(1)}, u32[]{:S(2)}, u32[]{:S(2)}) collective-permute-start(bf16[2,256,256]{1,2,0:T(8,128)(2,1)S(1)} %bitcast.28), channel_id=1, source_target_pairs={{0,64},{64,128},{128,192},{192,0},{1,65},{65,129},{129,193},{193,1... | collective-permute-start | bytes 786440 | tf_op jit(solution)/shard_map/ppermute | solution.py:114

commit v6 on v5

--- a/solution.py
+++ b/solution.py
@@ -8,7 +8,7 @@
 from jax.sharding import PartitionSpec as P
 
 LEFT_CHUNK = 16
-RIGHT_CHUNK = 32
+RIGHT_CHUNK = 16
 VMEM_LIMIT = 48 * 1024 * 1024
 
 
@@ -50,52 +50,114 @@
     )(dep, left_sector, tile_count, blocks, tiles)
 
 
-def _right_kernel(n_term, n_sector, arr_ref, rsel_ref, me_ref, a_ref, rt_ref, o_ref):
-    base = pl.program_id(0) * RIGHT_CHUNK
-    rows = o_ref.shape[1]
+def _right_kernel(n_term, n_sector, order_ref, ssec_ref, sarr_ref, me_ref, a_ref, rt_ref,
+                  o_hbm, obuf, sem):
+    c = pl.program_id(0)
+    steps = pl.num_programs(0)
+    base = c * RIGHT_CHUNK
+    rows = obuf.shape[2]
     per_term = a_ref.shape[0] // n_term
-    accs = [None] * n_sector
+    slot = lax.rem(c, 2)
+
+    def writes(step, buf):
+        return [
+            pltpu.make_async_copy(
+                obuf.at[buf, q], o_hbm.at[order_ref[step * RIGHT_CHUNK + q]], sem.at[buf, q]
+            )
+            for q in range(RIGHT_CHUNK)
+        ]
+
+    @pl.when(c >= 2)
+    def _():
+        for cp in writes(c - 2, slot):
+            cp.wait()
+
+    lhs = []
     for k in range(n_term):
         origin = lax.rem(me_ref[0] + (n_term - k), n_term) * per_term
-        lhs = jnp.concatenate(
-            [a_ref[origin + arr_ref[base + q]] for q in range(RIGHT_CHUNK)], axis=0
-        )
-        for sector in range(n_sector):
+        lhs.append(jnp.concatenate(
+            [a_ref[origin + sarr_ref[base + q]] for q in range(RIGHT_CHUNK)], axis=0
+        ))
+    first = ssec_ref[base]
+    mixed = first != ssec_ref[base + RIGHT_CHUNK - 1]
+
+    @pl.when(jnp.logical_not(mixed))
+    def _():
+        acc = None
+        for k in range(n_term):
             part = jnp.dot(
-                lhs, rt_ref[k * n_sector + sector], preferred_element_type=jnp.float32
+                lhs[k], rt_ref[k * n_sector + first], preferred_element_type=jnp.float32
             )
-            accs[sector] = part if accs[sector] is None else accs[sector] + part
-    for q in range(RIGHT_CHUNK):
-        chosen = rsel_ref[base + q]
-        out = accs[n_sector - 1][q * rows:(q + 1) * rows]
-        for sector in range(n_sector - 1):
-            out = jnp.where(chosen == sector, accs[sector][q * rows:(q + 1) * rows], out)
-        o_ref[q] = out.astype(o_ref.dtype)
+            acc = part if acc is None else acc + part
+        for q in range(RIGHT_CHUNK):
+            obuf[slot, q] = acc[q * rows:(q + 1) * rows].astype(obuf.dtype)
+
+    @pl.when(mixed)
+    def _():
+        accs = [None] * n_sector
+        for k in range(n_term):
+            for sector in range(n_sector):
+                part = jnp.dot(
+                    lhs[k], rt_ref[k * n_sector + sector], preferred_element_type=jnp.float32
+                )
+                accs[sector] = part if accs[sector] is None else accs[sector] + part
+        for q in range(RIGHT_CHUNK):
+            chosen = ssec_ref[base + q]
+            out = accs[n_sector - 1][q * rows:(q + 1) * rows]
+            for sector in range(n_sector - 1):
+                out = jnp.where(chosen == sector, accs[sector][q * rows:(q + 1) * rows], out)
+            obuf[slot, q] = out.astype(obuf.dtype)
+
+    for cp in writes(c, slot):
+        cp.start()
+
+    @pl.when(c == steps - 1)
+    def _():
+        @pl.when(c >= 1)
+        def _():
+            for cp in writes(c - 1, 1 - slot):
+                cp.wait()
+        for cp in writes(c, slot):
+            cp.wait()
 
 
 def apply_right(incoming, right_t, arr, rsel, me, n_term, n_sector):
     total, rows, w = incoming.shape
     n = arr.shape[0]
+    idx = jnp.arange(n, dtype=jnp.int32)
+    before = (rsel[None, :] < rsel[:, None]) | (
+        (rsel[None, :] == rsel[:, None]) & (idx[None, :] < idx[:, None])
+    )
+    position = jnp.sum(before.astype(jnp.int32), axis=1)
+    order = jnp.sum(jnp.where(position[None, :] == idx[:, None], idx[None, :], 0), axis=1)
+    ssec = jnp.take(rsel, order)
+    sarr = jnp.take(arr, order)
     spec = pltpu.PrefetchScalarGridSpec(
-        num_scalar_prefetch=3,
+        num_scalar_prefetch=4,
         grid=(n // RIGHT_CHUNK,),
         in_specs=[
             pl.BlockSpec(incoming.shape, lambda c, *_: (0, 0, 0)),
             pl.BlockSpec(right_t.shape, lambda c, *_: (0, 0, 0)),
         ],
-        out_specs=pl.BlockSpec((RIGHT_CHUNK, rows, w), lambda c, *_: (c, 0, 0)),
+        out_specs=pl.BlockSpec(memory_space=pl.ANY),
+        scratch_shapes=[
+            pltpu.VMEM((2, RIGHT_CHUNK, rows, w), jnp.bfloat16),
+            pltpu.SemaphoreType.DMA((2, RIGHT_CHUNK)),
+        ],
     )
     return pl.pallas_call(
         functools.partial(_right_kernel, n_term, n_sector),
         grid_spec=spec,
         out_shape=jax.ShapeDtypeStruct((n, rows, w), jnp.bfloat16),
-        compiler_params=pltpu.CompilerParams(vmem_limit_bytes=VMEM_LIMIT),
+        compiler_params=pltpu.CompilerParams(
+            vmem_limit_bytes=VMEM_LIMIT, dimension_semantics=("arbitrary",)
+        ),
         cost_estimate=pl.CostEstimate(
-            flops=2 * n_sector * total * rows * w * w,
+            flops=2 * total * rows * w * w,
             bytes_accessed=2 * (total * rows * w + right_t.size + n * rows * w),
             transcendentals=0,
         ),
-    )(arr, rsel, me, incoming, right_t)
+    )(order, ssec, sarr, me, incoming, right_t)
 
 
 def on_device(

time: 227 us -> 227 us (level)
  transfers between devices with their start and end apart: 4 -> 4, of which waited for: 4 -> 4; matrix products, arithmetic and copies ran while one was open for 0% -> 1% of each run, Pallas kernels for 0% -> 0%
where the time goes in v6:
time: 227 us; the launch traced here: 226 us
  waiting for transfers between devices  182 us (80%)
  starting transfers between devices  20.4 us (9%)
  Pallas kernels  18.3 us (8%)
  local copies, waits for them, and re-layouts  4.34 us (2%)
    all_to_all x1, waiting for transfers between devices, on_device(): lax.all_to_all(outgoing.reshape(n_term * tiles_dev, rows, width), ('term'...  150 us
    ppermute x3, waiting for transfers between devices, on_device(): right_parts.append(lax.ppermute(own_right_t, 'term', perm))  31.8 us
    all_to_all x1, starting transfers between devices, on_device(): lax.all_to_all(outgoing.reshape(n_term * tiles_dev, rows, width), ('term'...  16.6 us
    pallas_call x1, Pallas kernels, apply_right(): pl.pallas_call(functools.partial(_right_kernel, n_term, n_sector), grid_s...  9.48 us
    pallas_call x1, Pallas kernels, apply_left(): pl.pallas_call(_left_kernel, grid_spec=spec, out_shape=jax.ShapeDtypeStru...  8.79 us
  transfers between devices with their start and end apart: 4, of which 4 were waited for; matrix products, arithmetic and copies ran while one was open for 1% of the time, Pallas kernels for 0%

profile of v6, /device:TPU:1, one launch (start us, length us, event | category | flops | bytes accessed | tf_op | source)
XLA Modules:
  0.0 226.3 jit_solution(3979113435571186098)
XLA Ops:
  0.0 0.0 copy-start
  0.7 0.0 copy-start.1
  0.7 0.9 copy-done.1
  1.6 0.0 copy-start.2
  1.6 0.7 copy-done.2
  2.3 0.0 copy-start.3
  2.3 0.7 copy-done.3
  2.9 8.8 %shard_map.82 = bf16[4,64,64,256]{3,2,1,0:T(8,128)(2,1)} custom-call(s32[64]{0:T(128)S(1)} %bitcast.21, s32[64]{0:T(128)S(1)} %bitcast.22, s32[1]{0:T(128)S(6)} %copy.12.count_ref, bf16[2,256,256]{2,1,0:T(8,128)(2,1)S(1)} %bitcast.20, bf16[64,256,256]{2,1,0:T(8,128)(2,1)} %bitcast.26), custom_call_target="tpu_custom_call" | custom-call | flops 2147483648 | bytes 17039360 | tf_op jit(solution)/shard_map/pallas_call | solution.py:40
  11.7 0.0 copy-start.5
  11.7 0.0 copy-start.4
  11.7 16.6 %all-to-all-start = ((bf16[256,64,256]{2,1,0:T(8,128)(2,1)}), bf16[256,64,256]{2,1,0:T(8,128)(2,1)}, u32[]{:S(2)}, u32[]{:S(2)}) async-start(bf16[256,64,256]{2,1,0:T(8,128)(2,1)} %bitcast.25), calls=%async_computation | async-start | bytes 16777216 | tf_op jit(solution)/shard_map/all_to_all | solution.py:185
  28.4 0.0 copy-done.5
  28.4 2.6 %collective-permute-start.2 = (bf16[2,256,256]{1,2,0:T(8,128)(2,1)S(1)}, bf16[2,256,256]{1,2,0:T(8,128)(2,1)S(1)}, u32[]{:S(2)}, u32[]{:S(2)}) collective-permute-start(bf16[2,256,256]{1,2,0:T(8,128)(2,1)S(1)} %bitcast.27), channel_id=1, source_target_pairs={{0,192},{64,0},{128,64},{192,128},{1,193},{65,1},{129,65},{193,129... | collective-permute-start | bytes 786440 | tf_op jit(solution)/shard_map/ppermute | solution.py:176
  31.0 0.6 collective-permute-start.1
  31.6 0.6 collective-permute-start
  32.2 0.0 copy-done.4
  32.2 0.2 convert_reduce_fusion
  32.4 0.1 select_reduce_fusion.order_ref
  32.5 0.8 gather_fusion
  33.3 0.0 copy-done
  33.3 0.8 gather_fusion.1
  34.1 21.3 %collective-permute-done.2 = bf16[2,256,256]{1,2,0:T(8,128)(2,1)S(1)} collective-permute-done((bf16[2,256,256]{1,2,0:T(8,128)(2,1)S(1)}, bf16[2,256,256]{1,2,0:T(8,128)(2,1)S(1)}, u32[]{:S(2)}, u32[]{:S(2)}) %collective-permute-start.2) | collective-permute-done | bytes 262176 | tf_op jit(solution)/shard_map/ppermute | solution.py:176
  55.4 0.4 collective-permute-done.1
  55.8 10.1 %collective-permute-done = bf16[2,256,256]{1,2,0:T(8,128)(2,1)S(1)} collective-permute-done((bf16[2,256,256]{1,2,0:T(8,128)(2,1)S(1)}, bf16[2,256,256]{1,2,0:T(8,128)(2,1)S(1)}, u32[]{:S(2)}, u32[]{:S(2)}) %collective-permute-start) | collective-permute-done | bytes 262176 | tf_op jit(solution)/shard_map/ppermute | solution.py:176
  65.9 0.1 pad_maximum_fusion
  66.1 0.5 copy.11
  66.6 150.2 %all-to-all-done.a_ref = bf16[256,64,256]{2,1,0:T(8,128)(2,1)} async-done(((bf16[256,64,256]{2,1,0:T(8,128)(2,1)}), bf16[256,64,256]{2,1,0:T(8,128)(2,1)}, u32[]{:S(2)}, u32[]{:S(2)}) %all-to-all-start) | async-done | bytes 8388640 | tf_op jit(solution)/shard_map/all_to_all | solution.py:185
  216.8 9.5 %shard_map.83 = bf16[64,64,256]{2,1,0:T(8,128)(2,1)} custom-call(s32[64]{0:T(128)S(1)} %select_reduce_fusion.order_ref, s32[64]{0:T(128)S(1)} %get-tuple-element.7.ssec_ref, s32[64]{0:T(128)S(1)} %get-tuple-element.6.sarr_ref, s32[1]{0:T(128)} %bitcast.2.me_ref, bf16[256,64,256]{2,1,0:T(8,128)(2,1)} %all-to-all-done.a_ref, bf16[8,256,256]{2,1,0:T(8,128)(2,1)S(1)} %bitcast.19), custom_call_target="tpu_custom_call" | custom-call | flops 2147483648 | bytes 11534336 | tf_op jit(solution)/shard_map/pallas_call | solution.py:148
  (3 shorter events, 0.0 us)
Async XLA Ops:
  0.0 33.3 %copy-start = (s32[1,64]{1,0:T(1,128)S(1)}, s32[1,64]{1,0:T(1,128)}, u32[]{:S(2)}) copy-start(s32[1,64]{1,0:T(1,128)} %param.17) | copy-start | bytes 772
  0.7 1.0 copy-start.1
  1.6 0.7 copy-start.2
  2.3 0.7 copy-start.3
  11.7 16.7 %copy-start.5 = (bf16[1,2,256,256]{3,2,1,0:T(8,128)(2,1)S(1)}, bf16[1,2,256,256]{3,2,1,0:T(8,128)(2,1)}, u32[]{:S(2)}) copy-start(bf16[1,2,256,256]{3,2,1,0:T(8,128)(2,1)} %param.12) | copy-start | bytes 786436
  11.7 20.5 %copy-start.4 = (s32[1,64]{1,0:T(1,128)S(1)}, s32[1,64]{1,0:T(1,128)}, u32[]{:S(2)}) copy-start(s32[1,64]{1,0:T(1,128)} %param.14) | copy-start | bytes 772
  11.7 205.1 %all-to-all-start = ((bf16[256,64,256]{2,1,0:T(8,128)(2,1)}), bf16[256,64,256]{2,1,0:T(8,128)(2,1)}, u32[]{:S(2)}, u32[]{:S(2)}) async-start(bf16[256,64,256]{2,1,0:T(8,128)(2,1)} %bitcast.25), calls=%async_computation | async-start | bytes 16777216 | tf_op jit(solution)/shard_map/all_to_all | solution.py:185
  28.4 27.0 %collective-permute-start.2 = (bf16[2,256,256]{1,2,0:T(8,128)(2,1)S(1)}, bf16[2,256,256]{1,2,0:T(8,128)(2,1)S(1)}, u32[]{:S(2)}, u32[]{:S(2)}) collective-permute-start(bf16[2,256,256]{1,2,0:T(8,128)(2,1)S(1)} %bitcast.27), channel_id=1, source_target_pairs={{0,192},{64,0},{128,64},{192,128},{1,193},{65,1},{129,65},{193,129... | collective-permute-start | bytes 786440 | tf_op jit(solution)/shard_map/ppermute | solution.py:176
  31.0 24.8 %collective-permute-start.1 = (bf16[2,256,256]{1,2,0:T(8,128)(2,1)S(1)}, bf16[2,256,256]{1,2,0:T(8,128)(2,1)S(1)}, u32[]{:S(2)}, u32[]{:S(2)}) collective-permute-start(bf16[2,256,256]{1,2,0:T(8,128)(2,1)S(1)} %bitcast.28), channel_id=1, source_target_pairs={{0,128},{64,192},{128,0},{192,64},{1,129},{65,193},{129,1},{193,65... | collective-permute-start | bytes 786440 | tf_op jit(solution)/shard_map/ppermute | solution.py:176
  31.6 34.3 %collective-permute-start = (bf16[2,256,256]{1,2,0:T(8,128)(2,1)S(1)}, bf16[2,256,256]{1,2,0:T(8,128)(2,1)S(1)}, u32[]{:S(2)}, u32[]{:S(2)}) collective-permute-start(bf16[2,256,256]{1,2,0:T(8,128)(2,1)S(1)} %bitcast.29), channel_id=1, source_target_pairs={{0,64},{64,128},{128,192},{192,0},{1,65},{65,129},{129,193},{193,1... | collective-permute-start | bytes 786440 | tf_op jit(solution)/shard_map/ppermute | solution.py:176

commit v7 on v6

--- a/solution.py
+++ b/solution.py
@@ -12,42 +12,80 @@
 VMEM_LIMIT = 48 * 1024 * 1024
 
 
-def _left_kernel(dep_ref, sector_ref, count_ref, m_ref, x_ref, o_ref):
-    base = pl.program_id(0) * LEFT_CHUNK
-    n_term, _, rows, _ = o_ref.shape
-    for k in range(LEFT_CHUNK):
-        slot = dep_ref[base + k]
+def _left_kernel(n_tiles, meta_ref, m_ref, x_ref, o_hbm, obuf, sem):
+    c = pl.program_id(0)
+    steps = pl.num_programs(0)
+    base = c * LEFT_CHUNK
+    n_term, _, rows, _ = obuf.shape[1:]
+    slot = lax.rem(c, 2)
+
+    def writes(step, buf):
+        return [
+            pltpu.make_async_copy(
+                obuf.at[buf, :, q], o_hbm.at[:, meta_ref[step * LEFT_CHUNK + q]], sem.at[buf, q]
+            )
+            for q in range(LEFT_CHUNK)
+        ]
+
+    @pl.when(c >= 2)
+    def _():
+        for cp in writes(c - 2, slot):
+            cp.wait()
+
+    for q in range(LEFT_CHUNK):
+        tile = base + q
         prod = jnp.dot(
-            m_ref[sector_ref[slot]], x_ref[slot], preferred_element_type=jnp.float32
-        )
-        prod = jnp.where(slot < count_ref[0], prod, 0.0).astype(o_ref.dtype)
+            m_ref[meta_ref[n_tiles + tile]], x_ref[q], preferred_element_type=jnp.float32
+        )
+        prod = jnp.where(tile < meta_ref[2 * n_tiles], prod, 0.0).astype(obuf.dtype)
         for p in range(n_term):
-            o_ref[p, k] = prod[p * rows:(p + 1) * rows]
+            obuf[slot, p, q] = prod[p * rows:(p + 1) * rows]
+
+    for cp in writes(c, slot):
+        cp.start()
+
+    @pl.when(c == steps - 1)
+    def _():
+        @pl.when(c >= 1)
+        def _():
+            for cp in writes(c - 1, 1 - slot):
+                cp.wait()
+        for cp in writes(c, slot):
+            cp.wait()
 
 
 def apply_left(blocks, tiles, dep, left_sector, tile_count, n_term):
     n, w, _ = tiles.shape
     rows = w // n_term
+    idx = jnp.arange(n, dtype=jnp.int32)
+    position = jnp.sum(jnp.where(dep[None, :] == idx[:, None], idx[None, :], 0), axis=1)
+    meta = jnp.concatenate([position, left_sector, tile_count])
     spec = pltpu.PrefetchScalarGridSpec(
-        num_scalar_prefetch=3,
+        num_scalar_prefetch=1,
         grid=(n // LEFT_CHUNK,),
         in_specs=[
             pl.BlockSpec(blocks.shape, lambda c, *_: (0, 0, 0)),
-            pl.BlockSpec(tiles.shape, lambda c, *_: (0, 0, 0)),
-        ],
-        out_specs=pl.BlockSpec((n_term, LEFT_CHUNK, rows, w), lambda c, *_: (0, c, 0, 0)),
+            pl.BlockSpec((LEFT_CHUNK, w, w), lambda c, *_: (c, 0, 0)),
+        ],
+        out_specs=pl.BlockSpec(memory_space=pl.ANY),
+        scratch_shapes=[
+            pltpu.VMEM((2, n_term, LEFT_CHUNK, rows, w), jnp.bfloat16),
+            pltpu.SemaphoreType.DMA((2, LEFT_CHUNK)),
+        ],
     )
     return pl.pallas_call(
-        _left_kernel,
+        functools.partial(_left_kernel, n),
         grid_spec=spec,
         out_shape=jax.ShapeDtypeStruct((n_term, n, rows, w), jnp.bfloat16),
-        compiler_params=pltpu.CompilerParams(vmem_limit_bytes=VMEM_LIMIT),
+        compiler_params=pltpu.CompilerParams(
+            vmem_limit_bytes=VMEM_LIMIT, dimension_semantics=("arbitrary",)
+        ),
         cost_estimate=pl.CostEstimate(
             flops=2 * n * w * w * w,
             bytes_accessed=2 * (2 * n * w * w + blocks.size),
             transcendentals=0,
         ),
-    )(dep, left_sector, tile_count, blocks, tiles)
+    )(meta, blocks, tiles)
 
 
 def _right_kernel(n_term, n_sector, order_ref, ssec_ref, sarr_ref, me_ref, a_ref, rt_ref,

time: 227 us -> 227 us (level)
  no operation moved by 1% of the time
where the time goes in v7:
time: 227 us
  waiting for transfers between devices  182 us (80%)
  starting transfers between devices  20.4 us (9%)
  Pallas kernels  18.5 us (8%)
  local copies, waits for them, and re-layouts  3.04 us (1%)
    all_to_all x1, waiting for transfers between devices, on_device(): lax.all_to_all(outgoing.reshape(n_term * tiles_dev, rows, width), ('term'...  150 us
    ppermute x3, waiting for transfers between devices, on_device(): right_parts.append(lax.ppermute(own_right_t, 'term', perm))  31.8 us
    all_to_all x1, starting transfers between devices, on_device(): lax.all_to_all(outgoing.reshape(n_term * tiles_dev, rows, width), ('term'...  16.7 us
    pallas_call x1, Pallas kernels, apply_right(): pl.pallas_call(functools.partial(_right_kernel, n_term, n_sector), grid_s...  9.48 us
    pallas_call x1, Pallas kernels, apply_left(): pl.pallas_call(functools.partial(_left_kernel, n), grid_spec=spec, out_sh...  9.04 us
  transfers between devices with their start and end apart: 4, of which 4 were waited for; matrix products, arithmetic and copies ran while one was open for 1% of the time, Pallas kernels for 0%

profile of v7, /device:TPU:1, one launch (start us, length us, event | category | flops | bytes accessed | tf_op | source)
XLA Modules:
  0.0 226.8 jit_solution(3378111182633936395)
XLA Ops:
  0.0 0.0 copy-start
  0.7 0.8 select_reduce_fusion
  1.4 0.7 pad_add_fusion.meta_ref
  2.2 0.0 copy-start.1
  2.2 0.9 copy-done.1
  3.1 9.0 %shard_map.82 = bf16[4,64,64,256]{3,2,1,0:T(8,128)(2,1)} custom-call(s32[129]{0:T(256)S(1)} %pad_add_fusion.meta_ref, bf16[2,256,256]{2,1,0:T(8,128)(2,1)S(1)} %bitcast.20, bf16[64,256,256]{2,1,0:T(8,128)(2,1)} %bitcast.24), custom_call_target="tpu_custom_call" | custom-call | flops 2147483648 | bytes 17039360 | tf_op jit(solution)/shard_map/pallas_call | solution.py:76
  12.2 0.0 copy-start.3
  12.2 0.0 copy-start.2
  12.2 16.7 %all-to-all-start = ((bf16[256,64,256]{2,1,0:T(8,128)(2,1)}), bf16[256,64,256]{2,1,0:T(8,128)(2,1)}, u32[]{:S(2)}, u32[]{:S(2)}) async-start(bf16[256,64,256]{2,1,0:T(8,128)(2,1)} %bitcast.23), calls=%async_computation | async-start | bytes 16777216 | tf_op jit(solution)/shard_map/all_to_all | solution.py:223
  28.9 0.0 copy-done.3
  28.9 2.6 %collective-permute-start.2 = (bf16[2,256,256]{1,2,0:T(8,128)(2,1)S(1)}, bf16[2,256,256]{1,2,0:T(8,128)(2,1)S(1)}, u32[]{:S(2)}, u32[]{:S(2)}) collective-permute-start(bf16[2,256,256]{1,2,0:T(8,128)(2,1)S(1)} %bitcast.25), channel_id=1, source_target_pairs={{0,192},{64,0},{128,64},{192,128},{1,193},{65,1},{129,65},{193,129... | collective-permute-start | bytes 786440 | tf_op jit(solution)/shard_map/ppermute | solution.py:214
  31.5 0.6 collective-permute-start.1
  32.1 0.6 collective-permute-start
  32.7 0.0 copy-done.2
  32.7 0.2 convert_reduce_fusion
  32.8 0.1 select_reduce_fusion.1.order_ref
  33.0 0.8 gather_fusion
  33.8 0.0 copy-done
  33.8 0.8 gather_fusion.1
  34.6 21.3 %collective-permute-done.2 = bf16[2,256,256]{1,2,0:T(8,128)(2,1)S(1)} collective-permute-done((bf16[2,256,256]{1,2,0:T(8,128)(2,1)S(1)}, bf16[2,256,256]{1,2,0:T(8,128)(2,1)S(1)}, u32[]{:S(2)}, u32[]{:S(2)}) %collective-permute-start.2) | collective-permute-done | bytes 262176 | tf_op jit(solution)/shard_map/ppermute | solution.py:214
  55.9 0.4 collective-permute-done.1
  56.3 10.1 %collective-permute-done = bf16[2,256,256]{1,2,0:T(8,128)(2,1)S(1)} collective-permute-done((bf16[2,256,256]{1,2,0:T(8,128)(2,1)S(1)}, bf16[2,256,256]{1,2,0:T(8,128)(2,1)S(1)}, u32[]{:S(2)}, u32[]{:S(2)}) %collective-permute-start) | collective-permute-done | bytes 262176 | tf_op jit(solution)/shard_map/ppermute | solution.py:214
  66.4 0.1 pad_maximum_fusion
  66.5 0.5 copy.11
  67.1 150.2 %all-to-all-done.a_ref = bf16[256,64,256]{2,1,0:T(8,128)(2,1)} async-done(((bf16[256,64,256]{2,1,0:T(8,128)(2,1)}), bf16[256,64,256]{2,1,0:T(8,128)(2,1)}, u32[]{:S(2)}, u32[]{:S(2)}) %all-to-all-start) | async-done | bytes 8388640 | tf_op jit(solution)/shard_map/all_to_all | solution.py:223
  217.3 9.5 %shard_map.83 = bf16[64,64,256]{2,1,0:T(8,128)(2,1)} custom-call(s32[64]{0:T(128)S(1)} %select_reduce_fusion.1.order_ref, s32[64]{0:T(128)S(1)} %get-tuple-element.7.ssec_ref, s32[64]{0:T(128)S(1)} %get-tuple-element.6.sarr_ref, s32[1]{0:T(128)} %bitcast.2.me_ref, bf16[256,64,256]{2,1,0:T(8,128)(2,1)} %all-to-all-done.a_ref, bf16[8,256,256]{2,1,0:T(8,128)(2,1)S(1)} %bitcast.19), custom_call_target="tpu_custom_call" | custom-call | flops 2147483648 | bytes 11534336 | tf_op jit(solution)/shard_map/pallas_call | solution.py:186
  (3 shorter events, 0.0 us)
Async XLA Ops:
  0.0 33.8 %copy-start = (s32[1,64]{1,0:T(1,128)S(1)}, s32[1,64]{1,0:T(1,128)}, u32[]{:S(2)}) copy-start(s32[1,64]{1,0:T(1,128)} %param.17) | copy-start | bytes 772
  2.2 0.9 copy-start.1
  12.2 16.7 %copy-start.3 = (bf16[1,2,256,256]{3,2,1,0:T(8,128)(2,1)S(1)}, bf16[1,2,256,256]{3,2,1,0:T(8,128)(2,1)}, u32[]{:S(2)}) copy-start(bf16[1,2,256,256]{3,2,1,0:T(8,128)(2,1)} %param.12) | copy-start | bytes 786436
  12.2 20.5 %copy-start.2 = (s32[1,64]{1,0:T(1,128)S(1)}, s32[1,64]{1,0:T(1,128)}, u32[]{:S(2)}) copy-start(s32[1,64]{1,0:T(1,128)} %param.14) | copy-start | bytes 772
  12.2 205.1 %all-to-all-start = ((bf16[256,64,256]{2,1,0:T(8,128)(2,1)}), bf16[256,64,256]{2,1,0:T(8,128)(2,1)}, u32[]{:S(2)}, u32[]{:S(2)}) async-start(bf16[256,64,256]{2,1,0:T(8,128)(2,1)} %bitcast.23), calls=%async_computation | async-start | bytes 16777216 | tf_op jit(solution)/shard_map/all_to_all | solution.py:223
  28.9 27.0 %collective-permute-start.2 = (bf16[2,256,256]{1,2,0:T(8,128)(2,1)S(1)}, bf16[2,256,256]{1,2,0:T(8,128)(2,1)S(1)}, u32[]{:S(2)}, u32[]{:S(2)}) collective-permute-start(bf16[2,256,256]{1,2,0:T(8,128)(2,1)S(1)} %bitcast.25), channel_id=1, source_target_pairs={{0,192},{64,0},{128,64},{192,128},{1,193},{65,1},{129,65},{193,129... | collective-permute-start | bytes 786440 | tf_op jit(solution)/shard_map/ppermute | solution.py:214
  31.5 24.8 %collective-permute-start.1 = (bf16[2,256,256]{1,2,0:T(8,128)(2,1)S(1)}, bf16[2,256,256]{1,2,0:T(8,128)(2,1)S(1)}, u32[]{:S(2)}, u32[]{:S(2)}) collective-permute-start(bf16[2,256,256]{1,2,0:T(8,128)(2,1)S(1)} %bitcast.26), channel_id=1, source_target_pairs={{0,128},{64,192},{128,0},{192,64},{1,129},{65,193},{129,1},{193,65... | collective-permute-start | bytes 786440 | tf_op jit(solution)/shard_map/ppermute | solution.py:214
  32.1 34.3 %collective-permute-start = (bf16[2,256,256]{1,2,0:T(8,128)(2,1)S(1)}, bf16[2,256,256]{1,2,0:T(8,128)(2,1)S(1)}, u32[]{:S(2)}, u32[]{:S(2)}) collective-permute-start(bf16[2,256,256]{1,2,0:T(8,128)(2,1)S(1)} %bitcast.27), channel_id=1, source_target_pairs={{0,64},{64,128},{128,192},{192,0},{1,65},{65,129},{129,193},{193,1... | collective-permute-start | bytes 786440 | tf_op jit(solution)/shard_map/ppermute | solution.py:214

commit v8 on v6

--- a/solution.py
+++ b/solution.py
@@ -7,8 +7,8 @@
 from jax.experimental.pallas import tpu as pltpu
 from jax.sharding import PartitionSpec as P
 
-LEFT_CHUNK = 16
-RIGHT_CHUNK = 16
+LEFT_CHUNK = 32
+RIGHT_CHUNK = 32
 VMEM_LIMIT = 48 * 1024 * 1024
 
 

time: 227 us -> 227 us (level)
  no operation moved by 1% of the time
where the time goes in v8:
time: 227 us
  waiting for transfers between devices  182 us (80%)
  starting transfers between devices  20.4 us (9%)
  Pallas kernels  18.6 us (8%)
  local copies, waits for them, and re-layouts  4.34 us (2%)
    all_to_all x1, waiting for transfers between devices, on_device(): lax.all_to_all(outgoing.reshape(n_term * tiles_dev, rows, width), ('term'...  150 us
    ppermute x3, waiting for transfers between devices, on_device(): right_parts.append(lax.ppermute(own_right_t, 'term', perm))  31.8 us
    all_to_all x1, starting transfers between devices, on_device(): lax.all_to_all(outgoing.reshape(n_term * tiles_dev, rows, width), ('term'...  16.6 us
    pallas_call x1, Pallas kernels, apply_right(): pl.pallas_call(functools.partial(_right_kernel, n_term, n_sector), grid_s...  10.2 us
    pallas_call x1, Pallas kernels, apply_left(): pl.pallas_call(_left_kernel, grid_spec=spec, out_shape=jax.ShapeDtypeStru...  8.47 us
  transfers between devices with their start and end apart: 4, of which 4 were waited for; matrix products, arithmetic and copies ran while one was open for 1% of the time, Pallas kernels for 0%

profile of v8, /device:TPU:1, one launch (start us, length us, event | category | flops | bytes accessed | tf_op | source)
XLA Modules:
  0.0 226.6 jit_solution(1028286527992017174)
XLA Ops:
  0.0 0.0 copy-start
  0.7 0.0 copy-start.1
  0.7 0.9 copy-done.1
  1.6 0.0 copy-start.2
  1.6 0.7 copy-done.2
  2.3 0.0 copy-start.3
  2.3 0.7 copy-done.3
  2.9 8.5 %shard_map.82 = bf16[4,64,64,256]{3,2,1,0:T(8,128)(2,1)} custom-call(s32[64]{0:T(128)S(1)} %bitcast.21, s32[64]{0:T(128)S(1)} %bitcast.22, s32[1]{0:T(128)S(6)} %copy.12.count_ref, bf16[2,256,256]{2,1,0:T(8,128)(2,1)S(1)} %bitcast.20, bf16[64,256,256]{2,1,0:T(8,128)(2,1)} %bitcast.26), custom_call_target="tpu_custom_call" | custom-call | flops 2147483648 | bytes 17039360 | tf_op jit(solution)/shard_map/pallas_call | solution.py:40
  11.4 0.0 copy-start.5
  11.4 0.0 copy-start.4
  11.4 16.6 %all-to-all-start = ((bf16[256,64,256]{2,1,0:T(8,128)(2,1)}), bf16[256,64,256]{2,1,0:T(8,128)(2,1)}, u32[]{:S(2)}, u32[]{:S(2)}) async-start(bf16[256,64,256]{2,1,0:T(8,128)(2,1)} %bitcast.25), calls=%async_computation | async-start | bytes 16777216 | tf_op jit(solution)/shard_map/all_to_all | solution.py:185
  28.1 0.0 copy-done.5
  28.1 2.6 %collective-permute-start.2 = (bf16[2,256,256]{1,2,0:T(8,128)(2,1)S(1)}, bf16[2,256,256]{1,2,0:T(8,128)(2,1)S(1)}, u32[]{:S(2)}, u32[]{:S(2)}) collective-permute-start(bf16[2,256,256]{1,2,0:T(8,128)(2,1)S(1)} %bitcast.27), channel_id=1, source_target_pairs={{0,192},{64,0},{128,64},{192,128},{1,193},{65,1},{129,65},{193,129... | collective-permute-start | bytes 786440 | tf_op jit(solution)/shard_map/ppermute | solution.py:176
  30.7 0.6 collective-permute-start.1
  31.3 0.6 collective-permute-start
  31.9 0.0 copy-done.4
  31.9 0.2 convert_reduce_fusion
  32.0 0.1 select_reduce_fusion.order_ref
  32.2 0.8 gather_fusion
  33.0 0.0 copy-done
  33.0 0.8 gather_fusion.1
  33.8 21.3 %collective-permute-done.2 = bf16[2,256,256]{1,2,0:T(8,128)(2,1)S(1)} collective-permute-done((bf16[2,256,256]{1,2,0:T(8,128)(2,1)S(1)}, bf16[2,256,256]{1,2,0:T(8,128)(2,1)S(1)}, u32[]{:S(2)}, u32[]{:S(2)}) %collective-permute-start.2) | collective-permute-done | bytes 262176 | tf_op jit(solution)/shard_map/ppermute | solution.py:176
  55.0 0.4 collective-permute-done.1
  55.5 10.1 %collective-permute-done = bf16[2,256,256]{1,2,0:T(8,128)(2,1)S(1)} collective-permute-done((bf16[2,256,256]{1,2,0:T(8,128)(2,1)S(1)}, bf16[2,256,256]{1,2,0:T(8,128)(2,1)S(1)}, u32[]{:S(2)}, u32[]{:S(2)}) %collective-permute-start) | collective-permute-done | bytes 262176 | tf_op jit(solution)/shard_map/ppermute | solution.py:176
  65.6 0.1 pad_maximum_fusion
  65.7 0.5 copy.11
  66.3 150.2 %all-to-all-done.a_ref = bf16[256,64,256]{2,1,0:T(8,128)(2,1)} async-done(((bf16[256,64,256]{2,1,0:T(8,128)(2,1)}), bf16[256,64,256]{2,1,0:T(8,128)(2,1)}, u32[]{:S(2)}, u32[]{:S(2)}) %all-to-all-start) | async-done | bytes 8388640 | tf_op jit(solution)/shard_map/all_to_all | solution.py:185
  216.5 10.2 %shard_map.83 = bf16[64,64,256]{2,1,0:T(8,128)(2,1)} custom-call(s32[64]{0:T(128)S(1)} %select_reduce_fusion.order_ref, s32[64]{0:T(128)S(1)} %get-tuple-element.7.ssec_ref, s32[64]{0:T(128)S(1)} %get-tuple-element.6.sarr_ref, s32[1]{0:T(128)} %bitcast.2.me_ref, bf16[256,64,256]{2,1,0:T(8,128)(2,1)} %all-to-all-done.a_ref, bf16[8,256,256]{2,1,0:T(8,128)(2,1)S(1)} %bitcast.19), custom_call_target="tpu_custom_call" | custom-call | flops 2147483648 | bytes 11534336 | tf_op jit(solution)/shard_map/pallas_call | solution.py:148
  (3 shorter events, 0.0 us)
Async XLA Ops:
  0.0 33.0 %copy-start = (s32[1,64]{1,0:T(1,128)S(1)}, s32[1,64]{1,0:T(1,128)}, u32[]{:S(2)}) copy-start(s32[1,64]{1,0:T(1,128)} %param.17) | copy-start | bytes 772
  0.7 1.0 copy-start.1
  1.6 0.7 copy-start.2
  2.3 0.7 copy-start.3
  11.4 16.7 %copy-start.5 = (bf16[1,2,256,256]{3,2,1,0:T(8,128)(2,1)S(1)}, bf16[1,2,256,256]{3,2,1,0:T(8,128)(2,1)}, u32[]{:S(2)}) copy-start(bf16[1,2,256,256]{3,2,1,0:T(8,128)(2,1)} %param.12) | copy-start | bytes 786436
  11.4 20.5 %copy-start.4 = (s32[1,64]{1,0:T(1,128)S(1)}, s32[1,64]{1,0:T(1,128)}, u32[]{:S(2)}) copy-start(s32[1,64]{1,0:T(1,128)} %param.14) | copy-start | bytes 772
  11.4 205.1 %all-to-all-start = ((bf16[256,64,256]{2,1,0:T(8,128)(2,1)}), bf16[256,64,256]{2,1,0:T(8,128)(2,1)}, u32[]{:S(2)}, u32[]{:S(2)}) async-start(bf16[256,64,256]{2,1,0:T(8,128)(2,1)} %bitcast.25), calls=%async_computation | async-start | bytes 16777216 | tf_op jit(solution)/shard_map/all_to_all | solution.py:185
  28.1 27.0 %collective-permute-start.2 = (bf16[2,256,256]{1,2,0:T(8,128)(2,1)S(1)}, bf16[2,256,256]{1,2,0:T(8,128)(2,1)S(1)}, u32[]{:S(2)}, u32[]{:S(2)}) collective-permute-start(bf16[2,256,256]{1,2,0:T(8,128)(2,1)S(1)} %bitcast.27), channel_id=1, source_target_pairs={{0,192},{64,0},{128,64},{192,128},{1,193},{65,1},{129,65},{193,129... | collective-permute-start | bytes 786440 | tf_op jit(solution)/shard_map/ppermute | solution.py:176
  30.7 24.8 %collective-permute-start.1 = (bf16[2,256,256]{1,2,0:T(8,128)(2,1)S(1)}, bf16[2,256,256]{1,2,0:T(8,128)(2,1)S(1)}, u32[]{:S(2)}, u32[]{:S(2)}) collective-permute-start(bf16[2,256,256]{1,2,0:T(8,128)(2,1)S(1)} %bitcast.28), channel_id=1, source_target_pairs={{0,128},{64,192},{128,0},{192,64},{1,129},{65,193},{129,1},{193,65... | collective-permute-start | bytes 786440 | tf_op jit(solution)/shard_map/ppermute | solution.py:176
  31.3 34.3 %collective-permute-start = (bf16[2,256,256]{1,2,0:T(8,128)(2,1)S(1)}, bf16[2,256,256]{1,2,0:T(8,128)(2,1)S(1)}, u32[]{:S(2)}, u32[]{:S(2)}) collective-permute-start(bf16[2,256,256]{1,2,0:T(8,128)(2,1)S(1)} %bitcast.29), channel_id=1, source_target_pairs={{0,64},{64,128},{128,192},{192,0},{1,65},{65,129},{129,193},{193,1... | collective-permute-start | bytes 786440 | tf_op jit(solution)/shard_map/ppermute | solution.py:176

commit v9 on v6

--- a/solution.py
+++ b/solution.py
@@ -14,7 +14,7 @@
 
 def _left_kernel(dep_ref, sector_ref, count_ref, m_ref, x_ref, o_ref):
     base = pl.program_id(0) * LEFT_CHUNK
-    n_term, _, rows, _ = o_ref.shape
+    _, n_term, rows, _ = o_ref.shape
     for k in range(LEFT_CHUNK):
         slot = dep_ref[base + k]
         prod = jnp.dot(
@@ -22,7 +22,7 @@
         )
         prod = jnp.where(slot < count_ref[0], prod, 0.0).astype(o_ref.dtype)
         for p in range(n_term):
-            o_ref[p, k] = prod[p * rows:(p + 1) * rows]
+            o_ref[k, p] = prod[p * rows:(p + 1) * rows]
 
 
 def apply_left(blocks, tiles, dep, left_sector, tile_count, n_term):
@@ -35,12 +35,12 @@
             pl.BlockSpec(blocks.shape, lambda c, *_: (0, 0, 0)),
             pl.BlockSpec(tiles.shape, lambda c, *_: (0, 0, 0)),
         ],
-        out_specs=pl.BlockSpec((n_term, LEFT_CHUNK, rows, w), lambda c, *_: (0, c, 0, 0)),
+        out_specs=pl.BlockSpec((LEFT_CHUNK, n_term, rows, w), lambda c, *_: (c, 0, 0, 0)),
     )
     return pl.pallas_call(
         _left_kernel,
         grid_spec=spec,
-        out_shape=jax.ShapeDtypeStruct((n_term, n, rows, w), jnp.bfloat16),
+        out_shape=jax.ShapeDtypeStruct((n, n_term, rows, w), jnp.bfloat16),
         compiler_params=pltpu.CompilerParams(vmem_limit_bytes=VMEM_LIMIT),
         cost_estimate=pl.CostEstimate(
             flops=2 * n * w * w * w,
@@ -56,7 +56,6 @@
     steps = pl.num_programs(0)
     base = c * RIGHT_CHUNK
     rows = obuf.shape[2]
-    per_term = a_ref.shape[0] // n_term
     slot = lax.rem(c, 2)
 
     def writes(step, buf):
@@ -74,9 +73,9 @@
 
     lhs = []
     for k in range(n_term):
-        origin = lax.rem(me_ref[0] + (n_term - k), n_term) * per_term
+        origin = lax.rem(me_ref[0] + (n_term - k), n_term)
         lhs.append(jnp.concatenate(
-            [a_ref[origin + sarr_ref[base + q]] for q in range(RIGHT_CHUNK)], axis=0
+            [a_ref[sarr_ref[base + q] * n_term + origin] for q in range(RIGHT_CHUNK)], axis=0
         ))
     first = ssec_ref[base]
     mixed = first != ssec_ref[base + RIGHT_CHUNK - 1]
@@ -183,8 +182,8 @@
             left_env[0], vectors[v], departure[0], left_sector[0], tile_count, n_term
         )
         incoming = lax.all_to_all(
-            outgoing.reshape(n_term * tiles_dev, rows, width),
-            ("term", "sec"), split_axis=0, concat_axis=0, tiled=True,
+            outgoing.reshape(tiles_dev * n_term, rows, width),
+            ("sec", "term"), split_axis=0, concat_axis=0, tiled=True,
         )
         outs.append(
             apply_right(incoming, right_t, arrival[0], right_sector[0], me_arr, n_term, n_sector)

time: 227 us -> 227 us (level)
  transfers between devices with their start and end apart: 4 -> 4, of which waited for: 4 -> 3; matrix products, arithmetic and copies ran while one was open for 1% -> 1% of each run, Pallas kernels for 0% -> 0%
where the time goes in v9:
time: 227 us; the launch traced here: 226 us
  waiting for transfers between devices  182 us (80%)
  starting transfers between devices  20.4 us (9%)
  Pallas kernels  18.3 us (8%)
  local copies, waits for them, and re-layouts  4.34 us (2%)
    all_to_all x1, waiting for transfers between devices, on_device(): lax.all_to_all(outgoing.reshape(tiles_dev * n_term, rows, width), ('sec',...  150 us
    ppermute x3, waiting for transfers between devices, on_device(): right_parts.append(lax.ppermute(own_right_t, 'term', perm))  32 us
    all_to_all x1, starting transfers between devices, on_device(): lax.all_to_all(outgoing.reshape(tiles_dev * n_term, rows, width), ('sec',...  16.6 us
    pallas_call x1, Pallas kernels, apply_right(): pl.pallas_call(functools.partial(_right_kernel, n_term, n_sector), grid_s...  9.47 us
    pallas_call x1, Pallas kernels, apply_left(): pl.pallas_call(_left_kernel, grid_spec=spec, out_shape=jax.ShapeDtypeStru...  8.8 us
  transfers between devices with their start and end apart: 4, of which 3 were waited for; matrix products, arithmetic and copies ran while one was open for 1% of the time, Pallas kernels for 0%

profile of v9, /device:TPU:1, one launch (start us, length us, event | category | flops | bytes accessed | tf_op | source)
XLA Modules:
  0.0 226.5 jit_solution(7366519489705102801)
XLA Ops:
  0.0 0.0 copy-start
  0.7 0.0 copy-start.1
  0.7 0.9 copy-done.1
  1.6 0.0 copy-start.2
  1.6 0.7 copy-done.2
  2.3 0.0 copy-start.3
  2.3 0.7 copy-done.3
  2.9 8.8 %shard_map.82 = bf16[64,4,64,256]{3,2,1,0:T(8,128)(2,1)} custom-call(s32[64]{0:T(128)S(1)} %bitcast.21, s32[64]{0:T(128)S(1)} %bitcast.22, s32[1]{0:T(128)S(6)} %copy.12.count_ref, bf16[2,256,256]{2,1,0:T(8,128)(2,1)S(1)} %bitcast.20, bf16[64,256,256]{2,1,0:T(8,128)(2,1)} %bitcast.26), custom_call_target="tpu_custom_call" | custom-call | flops 2147483648 | bytes 17039360 | tf_op jit(solution)/shard_map/pallas_call | solution.py:40
  11.7 0.0 copy-start.5
  11.7 0.0 copy-start.4
  11.7 16.6 %all-to-all-start = ((bf16[256,64,256]{2,1,0:T(8,128)(2,1)}), bf16[256,64,256]{2,1,0:T(8,128)(2,1)}, u32[]{:S(2)}, u32[]{:S(2)}) async-start(bf16[256,64,256]{2,1,0:T(8,128)(2,1)} %bitcast.25), calls=%async_computation | async-start | bytes 16777216 | tf_op jit(solution)/shard_map/all_to_all | solution.py:184
  28.4 0.0 copy-done.5
  28.4 2.6 %collective-permute-start.2 = (bf16[2,256,256]{1,2,0:T(8,128)(2,1)S(1)}, bf16[2,256,256]{1,2,0:T(8,128)(2,1)S(1)}, u32[]{:S(2)}, u32[]{:S(2)}) collective-permute-start(bf16[2,256,256]{1,2,0:T(8,128)(2,1)S(1)} %bitcast.27), channel_id=1, source_target_pairs={{0,192},{64,0},{128,64},{192,128},{1,193},{65,1},{129,65},{193,129... | collective-permute-start | bytes 786440 | tf_op jit(solution)/shard_map/ppermute | solution.py:175
  31.0 0.6 collective-permute-start.1
  31.6 0.6 collective-permute-start
  32.2 0.0 copy-done.4
  32.2 0.2 convert_reduce_fusion
  32.4 0.1 select_reduce_fusion.order_ref
  32.5 0.8 gather_fusion
  33.3 0.0 copy-done
  33.3 0.8 gather_fusion.1
  34.1 23.1 %collective-permute-done.2 = bf16[2,256,256]{1,2,0:T(8,128)(2,1)S(1)} collective-permute-done((bf16[2,256,256]{1,2,0:T(8,128)(2,1)S(1)}, bf16[2,256,256]{1,2,0:T(8,128)(2,1)S(1)}, u32[]{:S(2)}, u32[]{:S(2)}) %collective-permute-start.2) | collective-permute-done | bytes 262176 | tf_op jit(solution)/shard_map/ppermute | solution.py:175
  57.2 0.0 collective-permute-done.1
  57.2 8.9 %collective-permute-done = bf16[2,256,256]{1,2,0:T(8,128)(2,1)S(1)} collective-permute-done((bf16[2,256,256]{1,2,0:T(8,128)(2,1)S(1)}, bf16[2,256,256]{1,2,0:T(8,128)(2,1)S(1)}, u32[]{:S(2)}, u32[]{:S(2)}) %collective-permute-start) | collective-permute-done | bytes 262176 | tf_op jit(solution)/shard_map/ppermute | solution.py:175
  66.1 0.1 pad_maximum_fusion
  66.2 0.5 copy.11
  66.8 150.3 %all-to-all-done.a_ref = bf16[256,64,256]{2,1,0:T(8,128)(2,1)} async-done(((bf16[256,64,256]{2,1,0:T(8,128)(2,1)}), bf16[256,64,256]{2,1,0:T(8,128)(2,1)}, u32[]{:S(2)}, u32[]{:S(2)}) %all-to-all-start) | async-done | bytes 8388640 | tf_op jit(solution)/shard_map/all_to_all | solution.py:184
  217.0 9.5 %shard_map.83 = bf16[64,64,256]{2,1,0:T(8,128)(2,1)} custom-call(s32[64]{0:T(128)S(1)} %select_reduce_fusion.order_ref, s32[64]{0:T(128)S(1)} %get-tuple-element.7.ssec_ref, s32[64]{0:T(128)S(1)} %get-tuple-element.6.sarr_ref, s32[1]{0:T(128)} %bitcast.2.me_ref, bf16[256,64,256]{2,1,0:T(8,128)(2,1)} %all-to-all-done.a_ref, bf16[8,256,256]{2,1,0:T(8,128)(2,1)S(1)} %bitcast.19), custom_call_target="tpu_custom_call" | custom-call | flops 2147483648 | bytes 11534336 | tf_op jit(solution)/shard_map/pallas_call | solution.py:147
  (3 shorter events, 0.0 us)
Async XLA Ops:
  0.0 33.3 %copy-start = (s32[1,64]{1,0:T(1,128)S(1)}, s32[1,64]{1,0:T(1,128)}, u32[]{:S(2)}) copy-start(s32[1,64]{1,0:T(1,128)} %param.17) | copy-start | bytes 772
  0.7 1.0 copy-start.1
  1.6 0.7 copy-start.2
  2.3 0.7 copy-start.3
  11.7 16.7 %copy-start.5 = (bf16[1,2,256,256]{3,2,1,0:T(8,128)(2,1)S(1)}, bf16[1,2,256,256]{3,2,1,0:T(8,128)(2,1)}, u32[]{:S(2)}) copy-start(bf16[1,2,256,256]{3,2,1,0:T(8,128)(2,1)} %param.12) | copy-start | bytes 786436
  11.7 20.5 %copy-start.4 = (s32[1,64]{1,0:T(1,128)S(1)}, s32[1,64]{1,0:T(1,128)}, u32[]{:S(2)}) copy-start(s32[1,64]{1,0:T(1,128)} %param.14) | copy-start | bytes 772
  11.7 205.3 %all-to-all-start = ((bf16[256,64,256]{2,1,0:T(8,128)(2,1)}), bf16[256,64,256]{2,1,0:T(8,128)(2,1)}, u32[]{:S(2)}, u32[]{:S(2)}) async-start(bf16[256,64,256]{2,1,0:T(8,128)(2,1)} %bitcast.25), calls=%async_computation | async-start | bytes 16777216 | tf_op jit(solution)/shard_map/all_to_all | solution.py:184
  28.4 28.8 %collective-permute-start.2 = (bf16[2,256,256]{1,2,0:T(8,128)(2,1)S(1)}, bf16[2,256,256]{1,2,0:T(8,128)(2,1)S(1)}, u32[]{:S(2)}, u32[]{:S(2)}) collective-permute-start(bf16[2,256,256]{1,2,0:T(8,128)(2,1)S(1)} %bitcast.27), channel_id=1, source_target_pairs={{0,192},{64,0},{128,64},{192,128},{1,193},{65,1},{129,65},{193,129... | collective-permute-start | bytes 786440 | tf_op jit(solution)/shard_map/ppermute | solution.py:175
  31.0 26.2 %collective-permute-start.1 = (bf16[2,256,256]{1,2,0:T(8,128)(2,1)S(1)}, bf16[2,256,256]{1,2,0:T(8,128)(2,1)S(1)}, u32[]{:S(2)}, u32[]{:S(2)}) collective-permute-start(bf16[2,256,256]{1,2,0:T(8,128)(2,1)S(1)} %bitcast.28), channel_id=1, source_target_pairs={{0,128},{64,192},{128,0},{192,64},{1,129},{65,193},{129,1},{193,65... | collective-permute-start | bytes 786440 | tf_op jit(solution)/shard_map/ppermute | solution.py:175
  31.6 34.5 %collective-permute-start = (bf16[2,256,256]{1,2,0:T(8,128)(2,1)S(1)}, bf16[2,256,256]{1,2,0:T(8,128)(2,1)S(1)}, u32[]{:S(2)}, u32[]{:S(2)}) collective-permute-start(bf16[2,256,256]{1,2,0:T(8,128)(2,1)S(1)} %bitcast.29), channel_id=1, source_target_pairs={{0,64},{64,128},{128,192},{192,0},{1,65},{65,129},{129,193},{193,1... | collective-permute-start | bytes 786440 | tf_op jit(solution)/shard_map/ppermute | solution.py:175

commit v10 on v6

--- a/solution.py
+++ b/solution.py
@@ -17,12 +17,20 @@
     n_term, _, rows, _ = o_ref.shape
     for k in range(LEFT_CHUNK):
         slot = dep_ref[base + k]
-        prod = jnp.dot(
-            m_ref[sector_ref[slot]], x_ref[slot], preferred_element_type=jnp.float32
-        )
-        prod = jnp.where(slot < count_ref[0], prod, 0.0).astype(o_ref.dtype)
-        for p in range(n_term):
-            o_ref[p, k] = prod[p * rows:(p + 1) * rows]
+        live = slot < count_ref[0]
+
+        @pl.when(live)
+        def _():
+            prod = jnp.dot(
+                m_ref[sector_ref[slot]], x_ref[slot], preferred_element_type=jnp.float32
+            ).astype(o_ref.dtype)
+            for p in range(n_term):
+                o_ref[p, k] = prod[p * rows:(p + 1) * rows]
+
+        @pl.when(jnp.logical_not(live))
+        def _():
+            for p in range(n_term):
+                o_ref[p, k] = jnp.zeros((rows, o_ref.shape[3]), o_ref.dtype)
 
 
 def apply_left(blocks, tiles, dep, left_sector, tile_count, n_term):

time: 227 us -> 235 us (1.035)
  Pallas kernels: 18.3 us -> 27.2 us
    pallas_call x1, Pallas kernels: 8.79 us -> 17.7 us  [apply_left(): pl.pallas_call(_left_kernel, grid_spec=spec, out_shape=jax.ShapeDtypeStru...]
where the time goes in v10:
time: 235 us
  waiting for transfers between devices  182 us (77%)
  Pallas kernels  27.2 us (12%)
  starting transfers between devices  20 us (9%)
  local copies, waits for them, and re-layouts  4.34 us (2%)
    all_to_all x1, waiting for transfers between devices, on_device(): lax.all_to_all(outgoing.reshape(n_term * tiles_dev, rows, width), ('term'...  150 us
    ppermute x3, waiting for transfers between devices, on_device(): right_parts.append(lax.ppermute(own_right_t, 'term', perm))  31.8 us
    pallas_call x1, Pallas kernels, apply_left(): pl.pallas_call(_left_kernel, grid_spec=spec, out_shape=jax.ShapeDtypeStru...  17.7 us
    all_to_all x1, starting transfers between devices, on_device(): lax.all_to_all(outgoing.reshape(n_term * tiles_dev, rows, width), ('term'...  16.2 us
    pallas_call x1, Pallas kernels, apply_right(): pl.pallas_call(functools.partial(_right_kernel, n_term, n_sector), grid_s...  9.49 us
  transfers between devices with their start and end apart: 4, of which 4 were waited for; matrix products, arithmetic and copies ran while one was open for 1% of the time, Pallas kernels for 0%

profile of v10, /device:TPU:1, one launch (start us, length us, event | category | flops | bytes accessed | tf_op | source)
XLA Modules:
  0.0 234.8 jit_solution(2111346378489070429)
XLA Ops:
  0.0 0.0 copy-start
  0.7 0.0 copy-start.1
  0.7 0.9 copy-done.1
  1.6 0.0 copy-start.2
  1.6 0.7 copy-done.2
  2.3 0.0 copy-start.3
  2.3 0.7 copy-done.3
  2.9 17.7 %shard_map.82 = bf16[4,64,64,256]{3,2,1,0:T(8,128)(2,1)} custom-call(s32[64]{0:T(128)S(1)} %bitcast.21, s32[64]{0:T(128)S(1)} %bitcast.22, s32[1]{0:T(128)S(6)} %copy.12.count_ref, bf16[2,256,256]{2,1,0:T(8,128)(2,1)S(1)} %bitcast.20, bf16[64,256,256]{2,1,0:T(8,128)(2,1)} %bitcast.26), custom_call_target="tpu_custom_call" | custom-call | flops 2147483648 | bytes 17039360 | tf_op jit(solution)/shard_map/pallas_call | solution.py:48
  20.7 0.0 copy-start.5
  20.7 0.0 copy-start.4
  20.7 16.2 %all-to-all-start = ((bf16[256,64,256]{2,1,0:T(8,128)(2,1)}), bf16[256,64,256]{2,1,0:T(8,128)(2,1)}, u32[]{:S(2)}, u32[]{:S(2)}) async-start(bf16[256,64,256]{2,1,0:T(8,128)(2,1)} %bitcast.25), calls=%async_computation | async-start | bytes 16777216 | tf_op jit(solution)/shard_map/all_to_all | solution.py:193
  36.9 0.0 copy-done.5
  36.9 2.6 %collective-permute-start.2 = (bf16[2,256,256]{1,2,0:T(8,128)(2,1)S(1)}, bf16[2,256,256]{1,2,0:T(8,128)(2,1)S(1)}, u32[]{:S(2)}, u32[]{:S(2)}) collective-permute-start(bf16[2,256,256]{1,2,0:T(8,128)(2,1)S(1)} %bitcast.27), channel_id=1, source_target_pairs={{0,192},{64,0},{128,64},{192,128},{1,193},{65,1},{129,65},{193,129... | collective-permute-start | bytes 786440 | tf_op jit(solution)/shard_map/ppermute | solution.py:184
  39.5 0.6 collective-permute-start.1
  40.1 0.6 collective-permute-start
  40.7 0.0 copy-done.4
  40.7 0.2 convert_reduce_fusion
  40.9 0.1 select_reduce_fusion.order_ref
  41.0 0.8 gather_fusion
  41.8 0.0 copy-done
  41.8 0.8 gather_fusion.1
  42.6 21.3 %collective-permute-done.2 = bf16[2,256,256]{1,2,0:T(8,128)(2,1)S(1)} collective-permute-done((bf16[2,256,256]{1,2,0:T(8,128)(2,1)S(1)}, bf16[2,256,256]{1,2,0:T(8,128)(2,1)S(1)}, u32[]{:S(2)}, u32[]{:S(2)}) %collective-permute-start.2) | collective-permute-done | bytes 262176 | tf_op jit(solution)/shard_map/ppermute | solution.py:184
  63.9 0.4 collective-permute-done.1
  64.3 10.1 %collective-permute-done = bf16[2,256,256]{1,2,0:T(8,128)(2,1)S(1)} collective-permute-done((bf16[2,256,256]{1,2,0:T(8,128)(2,1)S(1)}, bf16[2,256,256]{1,2,0:T(8,128)(2,1)S(1)}, u32[]{:S(2)}, u32[]{:S(2)}) %collective-permute-start) | collective-permute-done | bytes 262176 | tf_op jit(solution)/shard_map/ppermute | solution.py:184
  74.4 0.1 pad_maximum_fusion
  74.6 0.5 copy.11
  75.1 150.2 %all-to-all-done.a_ref = bf16[256,64,256]{2,1,0:T(8,128)(2,1)} async-done(((bf16[256,64,256]{2,1,0:T(8,128)(2,1)}), bf16[256,64,256]{2,1,0:T(8,128)(2,1)}, u32[]{:S(2)}, u32[]{:S(2)}) %all-to-all-start) | async-done | bytes 8388640 | tf_op jit(solution)/shard_map/all_to_all | solution.py:193
  225.3 9.5 %shard_map.83 = bf16[64,64,256]{2,1,0:T(8,128)(2,1)} custom-call(s32[64]{0:T(128)S(1)} %select_reduce_fusion.order_ref, s32[64]{0:T(128)S(1)} %get-tuple-element.7.ssec_ref, s32[64]{0:T(128)S(1)} %get-tuple-element.6.sarr_ref, s32[1]{0:T(128)} %bitcast.2.me_ref, bf16[256,64,256]{2,1,0:T(8,128)(2,1)} %all-to-all-done.a_ref, bf16[8,256,256]{2,1,0:T(8,128)(2,1)S(1)} %bitcast.19), custom_call_target="tpu_custom_call" | custom-call | flops 2147483648 | bytes 11534336 | tf_op jit(solution)/shard_map/pallas_call | solution.py:156
  (3 shorter events, 0.0 us)
Async XLA Ops:
  0.0 41.8 %copy-start = (s32[1,64]{1,0:T(1,128)S(1)}, s32[1,64]{1,0:T(1,128)}, u32[]{:S(2)}) copy-start(s32[1,64]{1,0:T(1,128)} %param.17) | copy-start | bytes 772
  0.7 1.0 copy-start.1
  1.6 0.7 copy-start.2
  2.3 0.7 copy-start.3
  20.7 16.2 %copy-start.5 = (bf16[1,2,256,256]{3,2,1,0:T(8,128)(2,1)S(1)}, bf16[1,2,256,256]{3,2,1,0:T(8,128)(2,1)}, u32[]{:S(2)}) copy-start(bf16[1,2,256,256]{3,2,1,0:T(8,128)(2,1)} %param.12) | copy-start | bytes 786436
  20.7 20.0 %copy-start.4 = (s32[1,64]{1,0:T(1,128)S(1)}, s32[1,64]{1,0:T(1,128)}, u32[]{:S(2)}) copy-start(s32[1,64]{1,0:T(1,128)} %param.14) | copy-start | bytes 772
  20.7 204.6 %all-to-all-start = ((bf16[256,64,256]{2,1,0:T(8,128)(2,1)}), bf16[256,64,256]{2,1,0:T(8,128)(2,1)}, u32[]{:S(2)}, u32[]{:S(2)}) async-start(bf16[256,64,256]{2,1,0:T(8,128)(2,1)} %bitcast.25), calls=%async_computation | async-start | bytes 16777216 | tf_op jit(solution)/shard_map/all_to_all | solution.py:193
  36.9 27.0 %collective-permute-start.2 = (bf16[2,256,256]{1,2,0:T(8,128)(2,1)S(1)}, bf16[2,256,256]{1,2,0:T(8,128)(2,1)S(1)}, u32[]{:S(2)}, u32[]{:S(2)}) collective-permute-start(bf16[2,256,256]{1,2,0:T(8,128)(2,1)S(1)} %bitcast.27), channel_id=1, source_target_pairs={{0,192},{64,0},{128,64},{192,128},{1,193},{65,1},{129,65},{193,129... | collective-permute-start | bytes 786440 | tf_op jit(solution)/shard_map/ppermute | solution.py:184
  39.5 24.8 %collective-permute-start.1 = (bf16[2,256,256]{1,2,0:T(8,128)(2,1)S(1)}, bf16[2,256,256]{1,2,0:T(8,128)(2,1)S(1)}, u32[]{:S(2)}, u32[]{:S(2)}) collective-permute-start(bf16[2,256,256]{1,2,0:T(8,128)(2,1)S(1)} %bitcast.28), channel_id=1, source_target_pairs={{0,128},{64,192},{128,0},{192,64},{1,129},{65,193},{129,1},{193,65... | collective-permute-start | bytes 786440 | tf_op jit(solution)/shard_map/ppermute | solution.py:184
  40.1 34.3 %collective-permute-start = (bf16[2,256,256]{1,2,0:T(8,128)(2,1)S(1)}, bf16[2,256,256]{1,2,0:T(8,128)(2,1)S(1)}, u32[]{:S(2)}, u32[]{:S(2)}) collective-permute-start(bf16[2,256,256]{1,2,0:T(8,128)(2,1)S(1)} %bitcast.29), channel_id=1, source_target_pairs={{0,64},{64,128},{128,192},{192,0},{1,65},{65,129},{129,193},{193,1... | collective-permute-start | bytes 786440 | tf_op jit(solution)/shard_map/ppermute | solution.py:184

commit v11 on v8

--- a/solution.py
+++ b/solution.py
@@ -7,7 +7,7 @@
 from jax.experimental.pallas import tpu as pltpu
 from jax.sharding import PartitionSpec as P
 
-LEFT_CHUNK = 32
+LEFT_CHUNK = 16
 RIGHT_CHUNK = 32
 VMEM_LIMIT = 48 * 1024 * 1024
 

time: 227 us -> 227 us (level)
  no operation moved by 1% of the time
where the time goes in v11:
time: 227 us
  waiting for transfers between devices  182 us (80%)
  starting transfers between devices  20.4 us (9%)
  Pallas kernels  18.9 us (8%)
  local copies, waits for them, and re-layouts  4.34 us (2%)
    all_to_all x1, waiting for transfers between devices, on_device(): lax.all_to_all(outgoing.reshape(n_term * tiles_dev, rows, width), ('term'...  150 us
    ppermute x3, waiting for transfers between devices, on_device(): right_parts.append(lax.ppermute(own_right_t, 'term', perm))  31.8 us
    all_to_all x1, starting transfers between devices, on_device(): lax.all_to_all(outgoing.reshape(n_term * tiles_dev, rows, width), ('term'...  16.6 us
    pallas_call x1, Pallas kernels, apply_right(): pl.pallas_call(functools.partial(_right_kernel, n_term, n_sector), grid_s...  10.2 us
    pallas_call x1, Pallas kernels, apply_left(): pl.pallas_call(_left_kernel, grid_spec=spec, out_shape=jax.ShapeDtypeStru...  8.79 us
  transfers between devices with their start and end apart: 4, of which 4 were waited for; matrix products, arithmetic and copies ran while one was open for 1% of the time, Pallas kernels for 0%

profile of v11, /device:TPU:1, one launch (start us, length us, event | category | flops | bytes accessed | tf_op | source)
XLA Modules:
  0.0 227.0 jit_solution(7132475922273274206)
XLA Ops:
  0.0 0.0 copy-start
  0.7 0.0 copy-start.1
  0.7 0.9 copy-done.1
  1.6 0.0 copy-start.2
  1.6 0.7 copy-done.2
  2.3 0.0 copy-start.3
  2.3 0.7 copy-done.3
  2.9 8.8 %shard_map.82 = bf16[4,64,64,256]{3,2,1,0:T(8,128)(2,1)} custom-call(s32[64]{0:T(128)S(1)} %bitcast.21, s32[64]{0:T(128)S(1)} %bitcast.22, s32[1]{0:T(128)S(6)} %copy.12.count_ref, bf16[2,256,256]{2,1,0:T(8,128)(2,1)S(1)} %bitcast.20, bf16[64,256,256]{2,1,0:T(8,128)(2,1)} %bitcast.26), custom_call_target="tpu_custom_call" | custom-call | flops 2147483648 | bytes 17039360 | tf_op jit(solution)/shard_map/pallas_call | solution.py:40
  11.7 0.0 copy-start.5
  11.7 0.0 copy-start.4
  11.7 16.6 %all-to-all-start = ((bf16[256,64,256]{2,1,0:T(8,128)(2,1)}), bf16[256,64,256]{2,1,0:T(8,128)(2,1)}, u32[]{:S(2)}, u32[]{:S(2)}) async-start(bf16[256,64,256]{2,1,0:T(8,128)(2,1)} %bitcast.25), calls=%async_computation | async-start | bytes 16777216 | tf_op jit(solution)/shard_map/all_to_all | solution.py:185
  28.4 0.0 copy-done.5
  28.4 2.6 %collective-permute-start.2 = (bf16[2,256,256]{1,2,0:T(8,128)(2,1)S(1)}, bf16[2,256,256]{1,2,0:T(8,128)(2,1)S(1)}, u32[]{:S(2)}, u32[]{:S(2)}) collective-permute-start(bf16[2,256,256]{1,2,0:T(8,128)(2,1)S(1)} %bitcast.27), channel_id=1, source_target_pairs={{0,192},{64,0},{128,64},{192,128},{1,193},{65,1},{129,65},{193,129... | collective-permute-start | bytes 786440 | tf_op jit(solution)/shard_map/ppermute | solution.py:176
  31.0 0.6 collective-permute-start.1
  31.6 0.6 collective-permute-start
  32.2 0.0 copy-done.4
  32.2 0.2 convert_reduce_fusion
  32.4 0.1 select_reduce_fusion.order_ref
  32.5 0.8 gather_fusion
  33.3 0.0 copy-done
  33.3 0.8 gather_fusion.1
  34.1 21.3 %collective-permute-done.2 = bf16[2,256,256]{1,2,0:T(8,128)(2,1)S(1)} collective-permute-done((bf16[2,256,256]{1,2,0:T(8,128)(2,1)S(1)}, bf16[2,256,256]{1,2,0:T(8,128)(2,1)S(1)}, u32[]{:S(2)}, u32[]{:S(2)}) %collective-permute-start.2) | collective-permute-done | bytes 262176 | tf_op jit(solution)/shard_map/ppermute | solution.py:176
  55.4 0.4 collective-permute-done.1
  55.8 10.1 %collective-permute-done = bf16[2,256,256]{1,2,0:T(8,128)(2,1)S(1)} collective-permute-done((bf16[2,256,256]{1,2,0:T(8,128)(2,1)S(1)}, bf16[2,256,256]{1,2,0:T(8,128)(2,1)S(1)}, u32[]{:S(2)}, u32[]{:S(2)}) %collective-permute-start) | collective-permute-done | bytes 262176 | tf_op jit(solution)/shard_map/ppermute | solution.py:176
  65.9 0.1 pad_maximum_fusion
  66.1 0.5 copy.11
  66.6 150.2 %all-to-all-done.a_ref = bf16[256,64,256]{2,1,0:T(8,128)(2,1)} async-done(((bf16[256,64,256]{2,1,0:T(8,128)(2,1)}), bf16[256,64,256]{2,1,0:T(8,128)(2,1)}, u32[]{:S(2)}, u32[]{:S(2)}) %all-to-all-start) | async-done | bytes 8388640 | tf_op jit(solution)/shard_map/all_to_all | solution.py:185
  216.8 10.2 %shard_map.83 = bf16[64,64,256]{2,1,0:T(8,128)(2,1)} custom-call(s32[64]{0:T(128)S(1)} %select_reduce_fusion.order_ref, s32[64]{0:T(128)S(1)} %get-tuple-element.7.ssec_ref, s32[64]{0:T(128)S(1)} %get-tuple-element.6.sarr_ref, s32[1]{0:T(128)} %bitcast.2.me_ref, bf16[256,64,256]{2,1,0:T(8,128)(2,1)} %all-to-all-done.a_ref, bf16[8,256,256]{2,1,0:T(8,128)(2,1)S(1)} %bitcast.19), custom_call_target="tpu_custom_call" | custom-call | flops 2147483648 | bytes 11534336 | tf_op jit(solution)/shard_map/pallas_call | solution.py:148
  (3 shorter events, 0.0 us)
Async XLA Ops:
  0.0 33.3 %copy-start = (s32[1,64]{1,0:T(1,128)S(1)}, s32[1,64]{1,0:T(1,128)}, u32[]{:S(2)}) copy-start(s32[1,64]{1,0:T(1,128)} %param.17) | copy-start | bytes 772
  0.7 1.0 copy-start.1
  1.6 0.7 copy-start.2
  2.3 0.7 copy-start.3
  11.7 16.7 %copy-start.5 = (bf16[1,2,256,256]{3,2,1,0:T(8,128)(2,1)S(1)}, bf16[1,2,256,256]{3,2,1,0:T(8,128)(2,1)}, u32[]{:S(2)}) copy-start(bf16[1,2,256,256]{3,2,1,0:T(8,128)(2,1)} %param.12) | copy-start | bytes 786436
  11.7 20.5 %copy-start.4 = (s32[1,64]{1,0:T(1,128)S(1)}, s32[1,64]{1,0:T(1,128)}, u32[]{:S(2)}) copy-start(s32[1,64]{1,0:T(1,128)} %param.14) | copy-start | bytes 772
  11.7 205.1 %all-to-all-start = ((bf16[256,64,256]{2,1,0:T(8,128)(2,1)}), bf16[256,64,256]{2,1,0:T(8,128)(2,1)}, u32[]{:S(2)}, u32[]{:S(2)}) async-start(bf16[256,64,256]{2,1,0:T(8,128)(2,1)} %bitcast.25), calls=%async_computation | async-start | bytes 16777216 | tf_op jit(solution)/shard_map/all_to_all | solution.py:185
  28.4 27.0 %collective-permute-start.2 = (bf16[2,256,256]{1,2,0:T(8,128)(2,1)S(1)}, bf16[2,256,256]{1,2,0:T(8,128)(2,1)S(1)}, u32[]{:S(2)}, u32[]{:S(2)}) collective-permute-start(bf16[2,256,256]{1,2,0:T(8,128)(2,1)S(1)} %bitcast.27), channel_id=1, source_target_pairs={{0,192},{64,0},{128,64},{192,128},{1,193},{65,1},{129,65},{193,129... | collective-permute-start | bytes 786440 | tf_op jit(solution)/shard_map/ppermute | solution.py:176
  31.0 24.8 %collective-permute-start.1 = (bf16[2,256,256]{1,2,0:T(8,128)(2,1)S(1)}, bf16[2,256,256]{1,2,0:T(8,128)(2,1)S(1)}, u32[]{:S(2)}, u32[]{:S(2)}) collective-permute-start(bf16[2,256,256]{1,2,0:T(8,128)(2,1)S(1)} %bitcast.28), channel_id=1, source_target_pairs={{0,128},{64,192},{128,0},{192,64},{1,129},{65,193},{129,1},{193,65... | collective-permute-start | bytes 786440 | tf_op jit(solution)/shard_map/ppermute | solution.py:176
  31.6 34.3 %collective-permute-start = (bf16[2,256,256]{1,2,0:T(8,128)(2,1)S(1)}, bf16[2,256,256]{1,2,0:T(8,128)(2,1)S(1)}, u32[]{:S(2)}, u32[]{:S(2)}) collective-permute-start(bf16[2,256,256]{1,2,0:T(8,128)(2,1)S(1)} %bitcast.29), channel_id=1, source_target_pairs={{0,64},{64,128},{128,192},{192,0},{1,65},{65,129},{129,193},{193,1... | collective-permute-start | bytes 786440 | tf_op jit(solution)/shard_map/ppermute | solution.py:176
